TPU v7x, 32 devices: a whole 2x2x4 slice. The times are simulated.
32 devices in a mesh: dp: 2 (over x), seq: 8 (over z, y), tensor: 2 (over core).
Axes of the slice: x: 2, y: 2, z: 4, core: 2. Of those that a mesh axis runs over, the one named last changes fastest.
Arguments:
- queries: bfloat16 [2, 1024, 1536], P('dp', 'seq', 'tensor')
- keys: bfloat16 [2, 1024, 1536], P('dp', 'seq', 'tensor')
- values: bfloat16 [2, 1024, 1536], P('dp', 'seq', 'tensor'), may hold values from -6 to 6
- out_weight: bfloat16 [1536, 1536], P('tensor'), may hold values from -0.15625 to 0.15625
- residual: bfloat16 [2, 1024, 1536], P('dp', 'seq', 'tensor'), may hold values from -1.1953125 to 1.1953125
- lengths: int32 [2], P('dp'), may hold values from 512 to 1024
- grad_out: bfloat16 [2, 1024, 1536], P('dp', 'seq', 'tensor'), may hold values from -6 to 6
Outputs:
- block_out: bfloat16 [2, 1024, 1536], P('dp', 'seq', 'tensor')
- grad_queries: bfloat16 [2, 1024, 1536], P('dp', 'seq', 'tensor')
- grad_keys: bfloat16 [2, 1024, 1536], P('dp', 'seq', 'tensor')
- grad_values: bfloat16 [2, 1024, 1536], P('dp', 'seq', 'tensor')
- grad_weight: float32 [1536, 1536], P('tensor', ('dp', 'seq'))
Inputs may be any that keep to these rules, and one draw needn't show every extreme that they name: Frames at positions from lengths[b] on are padding.
All inputs are finite; a program needn't handle non-finite values.
Results may differ from a plain program's by a relative error of at most 0.014.
Values may be sent and summed in bfloat16 or wider, within the bound.
No kernel may reach another device: no remote copies, remote signals or barrier semaphores. Data moves between devices by JAX's collectives and lax.ppermute only.
A program may use at most 64 MiB of HBM per device.

v0:
```python
import math

import jax
import jax.numpy as jnp
from jax import lax
from jax.sharding import PartitionSpec as P

HEAD_DIM = 96


block_rows = 1024


def split_heads(rows):
    return rows.reshape(rows.shape[0], -1, HEAD_DIM)


def join_heads(blocks):
    return jnp.transpose(blocks, (1, 0, 2)).reshape(blocks.shape[1], -1)


def by_blocks(step_fn, carry, piece):
    count = piece[0].shape[0]
    size = count if count <= block_rows else math.gcd(count, block_rows)

    def one(index, state):
        first = index * size
        part = tuple((lax.dynamic_slice_in_dim(item, first, size, 0) for item in piece))
        return step_fn(state, part, first)

    return lax.fori_loop(0, count // size, one, carry)


def shards(queries, keys, values, out_weight, residual, lengths, grad_out):
    scale = 1.0 / math.sqrt(HEAD_DIM)
    highest = lax.Precision.HIGHEST
    own_q = queries[0]
    own_k = keys[0]
    own_v = values[0]
    frames_here = own_q.shape[0]
    length = lengths[0]
    q_heads = split_heads(own_q)
    k_heads = split_heads(own_k)
    v_heads = split_heads(own_v)
    heads_here = q_heads.shape[1]
    key_pos = lax.axis_index("seq") * frames_here + jnp.arange(frames_here, dtype=jnp.int32)

    def masked_scores(left, right, positions):
        s = jnp.einsum("ihc,jhc->hij", left, right, preferred_element_type=jnp.float32) * scale
        return jnp.where(positions[None, None, :] < length, s, -1e30)

    def forward_step(state, part, start):
        run_max, run_sum, total = state
        k_rows, v_rows = part
        positions = start + jnp.arange(k_rows.shape[0], dtype=jnp.int32)
        s = masked_scores(q_heads, split_heads(k_rows), positions)
        new_max = jnp.maximum(run_max, jnp.max(s, axis=2))
        factor = jnp.exp(run_max - new_max)
        weights = jnp.exp(s - new_max[:, :, None])
        run_sum = run_sum * factor + jnp.sum(weights, axis=2)
        total = total * factor[:, :, None] + jnp.einsum(
            "hij,jhc->hic", weights, split_heads(v_rows).astype(jnp.float32), precision=highest
        )
        return (new_max, run_sum, total)

    start_state = (
        jnp.full((heads_here, frames_here), -1e30, jnp.float32),
        jnp.zeros((heads_here, frames_here), jnp.float32),
        jnp.zeros((heads_here, frames_here, HEAD_DIM), jnp.float32),
    )
    run_max, run_sum, total = by_blocks(
        forward_step,
        start_state,
        (
            lax.all_gather(own_k, "seq", axis=0, tiled=True),
            lax.all_gather(own_v, "seq", axis=0, tiled=True),
        ),
    )
    log_sum = run_max + jnp.log(run_sum)
    attn_full = total / run_sum[:, :, None]
    attn = join_heads(attn_full).astype(jnp.bfloat16)
    partial_out = jnp.dot(attn, out_weight, preferred_element_type=jnp.float32)
    mixed = lax.psum_scatter(
        partial_out.astype(jnp.bfloat16), "tensor", scatter_dimension=1, tiled=True
    ).astype(jnp.float32)
    block_out = (residual[0].astype(jnp.float32) + mixed).astype(jnp.bfloat16)
    grad_full = lax.all_gather(grad_out[0], "tensor", axis=1, tiled=True)
    grad_attn = lax.dot_general(
        grad_full, out_weight, (((1,), (1,)), ((), ())), preferred_element_type=jnp.float32
    ).astype(jnp.bfloat16)
    weight_term = lax.dot_general(
        attn, grad_full, (((0,), (0,)), ((), ())), preferred_element_type=jnp.float32
    )
    grad_weight = lax.psum_scatter(weight_term, ("dp", "seq"), scatter_dimension=1, tiled=True)
    g_heads = split_heads(grad_attn)
    delta = jnp.sum(jnp.transpose(g_heads, (1, 0, 2)).astype(jnp.float32) * attn_full, axis=2)

    def query_step(grad_q, part, start):
        k_rows, v_rows = part
        positions = start + jnp.arange(k_rows.shape[0], dtype=jnp.int32)
        s = masked_scores(q_heads, split_heads(k_rows), positions)
        probs = jnp.exp(s - log_sum[:, :, None])
        dots = jnp.einsum(
            "ihc,jhc->hij", g_heads, split_heads(v_rows), preferred_element_type=jnp.float32
        )
        dscores = (probs * (dots - delta[:, :, None]) * scale).astype(jnp.bfloat16)
        return grad_q + jnp.einsum(
            "hij,jhc->hic", dscores, split_heads(k_rows), preferred_element_type=jnp.float32
        )

    empty_q = jnp.zeros((heads_here, frames_here, HEAD_DIM), jnp.float32)
    grad_q = by_blocks(
        query_step,
        empty_q,
        (
            lax.all_gather(own_k, "seq", axis=0, tiled=True),
            lax.all_gather(own_v, "seq", axis=0, tiled=True),
        ),
    )

    def key_step(state, part, start):
        grad_k, grad_v = state
        q_rows, g_rows, lse_rows, delta_rows = part
        q_part = split_heads(q_rows.astype(jnp.bfloat16))
        g_part = split_heads(g_rows.astype(jnp.bfloat16))
        s = masked_scores(q_part, k_heads, key_pos)
        probs = jnp.exp(s - lse_rows.T[:, :, None])
        dots = jnp.einsum("ihc,jhc->hij", g_part, v_heads, preferred_element_type=jnp.float32)
        dscores = (probs * (dots - delta_rows.T[:, :, None]) * scale).astype(jnp.bfloat16)
        grad_k = grad_k + jnp.einsum(
            "hij,ihc->hjc", dscores, q_part, preferred_element_type=jnp.float32
        )
        grad_v = grad_v + jnp.einsum(
            "hij,ihc->hjc", probs.astype(jnp.bfloat16), g_part, preferred_element_type=jnp.float32
        )
        return (grad_k, grad_v)

    grad_k, grad_v = by_blocks(
        key_step,
        (empty_q, empty_q),
        (
            lax.all_gather(own_q.astype(jnp.float32), "seq", axis=0, tiled=True),
            lax.all_gather(grad_attn.astype(jnp.float32), "seq", axis=0, tiled=True),
            lax.all_gather(log_sum.T, "seq", axis=0, tiled=True),
            lax.all_gather(delta.T, "seq", axis=0, tiled=True),
        ),
    )
    return (
        block_out[None],
        join_heads(grad_q).astype(jnp.bfloat16)[None],
        join_heads(grad_k).astype(jnp.bfloat16)[None],
        join_heads(grad_v).astype(jnp.bfloat16)[None],
        grad_weight,
    )


def solution(mesh):
    in_specs = (
        P("dp", "seq", "tensor"),
        P("dp", "seq", "tensor"),
        P("dp", "seq", "tensor"),
        P("tensor", None),
        P("dp", "seq", "tensor"),
        P("dp"),
        P("dp", "seq", "tensor"),
    )
    out_specs = (
        P("dp", "seq", "tensor"),
        P("dp", "seq", "tensor"),
        P("dp", "seq", "tensor"),
        P("dp", "seq", "tensor"),
        P("tensor", ("dp", "seq")),
    )
    return jax.shard_map(shards, mesh=mesh, in_specs=in_specs, out_specs=out_specs, check_vma=False)
```

profile of v0, /device:TPU:0, one launch (start us, length us, event | category | flops | bytes accessed | tf_op | source)
XLA Modules:
  0.0 353.2 jit_solution(14263493875072485095)
XLA Ops:
  7.2 0.7 all-gather.11.cloned.1.call-update
  8.0 0.7 all-gather.13.cloned.1.call-update
  8.7 0.7 all-gather.15.cloned.1.call-update
  9.5 2.4 all-gather.2
  11.9 1.6 convolution_convert_fusion.1
  13.5 0.2 copy.22
  14.4 42.8 %all-gather.11.cloned.1.call-done = bf16[1,1024,768]{2,1,0:T(8,128)(2,1)} async-done(((bf16[1,128,768]{2,1,0:T(8,128)(2,1)}), bf16[1,1024,768]{2,1,0:T(8,128)(2,1)}) %all-gather.11.cloned.1.call-update) | async-done | bytes 1572880 | tf_op jit(solution)/shard_map/all_gather | solution.py:75
  57.1 2.6 copy.23
  59.8 42.1 %all-gather.13.cloned.1.call-done = bf16[1,1024,768]{2,1,0:T(8,128)(2,1)} async-done(((bf16[1,128,768]{2,1,0:T(8,128)(2,1)}), bf16[1,1024,768]{2,1,0:T(8,128)(2,1)}) %all-gather.13.cloned.1.call-update) | async-done | bytes 1572880 | tf_op jit(solution)/shard_map/all_gather | solution.py:76
  101.9 2.6 copy.24
  104.5 2.5 fusion.3
  107.0 1.0 fusion
  108.0 3.2 fusion.27
  111.2 1.3 convolution_convert_fusion
  112.5 3.0 fusion.23
  115.5 0.9 copy-done.2
  117.0 0.5 add_compare_fusion
  117.6 5.4 %fusion.16 = bf16[8,128,96]{1,2,0:T(8,128)(2,1)S(1)} fusion(bf16[1024,8,96]{0,2,1:T(8,128)(2,1)} %bitcast.76, f32[8,128,1024]{2,1,0:T(8,128)} %copy-done.1, bf16[128,8,96]{0,2,1:T(8,128)(2,1)S(1)} %bitcast.88, bf16[1024,8,96]{0,2,1:T(8,128)(2,1)} %bitcast.79, f32[8,128]{1,0:T(8,128)S(1)} %fusion.22, f32[8,128]{1,0:T(8,128)S(1)} %get-tuple-element.86, ...), kind=kOutput, calls=%fused_computation.21 | convolution fusion | flops 410091520 | bytes 7742464 | tf_op jit(solution)/shard_map/while/body/eval_jaxpr/hij,jhc->hic/dot_general | solution.py:107
  122.9 0.8 copy.30
  123.8 22.9 %all-gather.15.cloned.1.call-done = bf16[1,1024,768]{2,1,0:T(8,128)(2,1)} async-done(((bf16[1,128,768]{2,1,0:T(8,128)(2,1)}), bf16[1,1024,768]{2,1,0:T(8,128)(2,1)}) %all-gather.15.cloned.1.call-update) | async-done | bytes 1572880 | tf_op jit(solution)/shard_map/all_gather | solution.py:142
  146.7 2.6 copy.26
  149.3 42.5 %all-gather.9.cloned.1.call-done = bf16[1024,768]{1,0:T(8,128)(2,1)} async-done(((bf16[128,768]{1,0:T(8,128)(2,1)}), bf16[1024,768]{1,0:T(8,128)(2,1)}) %all-gather.9.cloned.1.call-update) | async-done | bytes 1572880 | tf_op jit(solution)/shard_map/all_gather | solution.py:143
  191.8 2.6 copy.28
  194.4 30.7 %all_gather.29 = f32[1024,8]{0,1:T(8,128)S(1)} all-gather(f32[128,8]{0,1:T(8,128)S(1)} %bitcast.96), channel_id=1, replica_groups=mesh['dp'=2,'seq'=8,'tensor'=2] {'seq'}, dimensions={0}, use_global_device_ids=true | all-gather | bytes 36864 | tf_op jit(solution)/shard_map/all_gather | solution.py:145
  225.1 30.8 %all_gather.27 = f32[1024,8]{0,1:T(8,128)S(1)} all-gather(f32[128,8]{0,1:T(8,128)S(1)} %get-tuple-element.84), channel_id=1, replica_groups=mesh['dp'=2,'seq'=8,'tensor'=2] {'seq'}, dimensions={0}, use_global_device_ids=true | all-gather | bytes 36864 | tf_op jit(solution)/shard_map/all_gather | solution.py:144
  255.9 4.2 %fusion.40 = f32[8,1024,128]{2,1,0:T(8,128)} fusion(bf16[1024,8,96]{0,2,1:T(8,128)(2,1)} %bitcast.77, bf16[128,8,96]{0,2,1:T(8,128)(2,1)S(1)} %bitcast.85), kind=kOutput, calls=%fused_computation.55 | convolution fusion | flops 201326592 | bytes 5963776 | tf_op jit(solution)/shard_map/while/body/eval_jaxpr/ihc,jhc->hij/dot_general | solution.py:49
  260.2 6.3 %fusion.17 = bf16[8,128,96]{1,2,0:T(8,128)(2,1)S(1)} fusion(bf16[1024,8,96]{0,2,1:T(8,128)(2,1)} %bitcast.78, f32[8,1024,128]{2,1,0:T(8,128)} %fusion.40, bf16[1024,8,96]{0,2,1:T(8,128)(2,1)} %bitcast.81, bf16[128,8,96]{0,2,1:T(8,128)(2,1)S(1)} %bitcast.89, f32[8,1024]{1,0:T(8,128)S(1)} %bitcast.95, f32[8,1024]{1,0:T(8,128)S(1)} %bitcast.93, ...), kind=kOutput, calls=%fused_computation.22 | convolution fusion | flops 410091520 | bytes 7798912 | tf_op jit(solution)/shard_map/while/body/eval_jaxpr/hij,ihc->hjc/dot_general | solution.py:130
  266.5 0.8 copy.31
  267.3 3.6 %fusion.18 = bf16[8,128,96]{1,2,0:T(8,128)(2,1)S(1)} fusion(bf16[1024,8,96]{0,2,1:T(8,128)(2,1)} %bitcast.82, f32[8,1024,128]{2,1,0:T(8,128)} %fusion.40, f32[8,1024]{1,0:T(8,128)S(1)} %bitcast.94, pred[128]{0:T(512)(128)(4,1)S(1)} %copy-done.9), kind=kOutput, calls=%fused_computation.23 | convolution fusion | flops 205619200 | bytes 5996672 | tf_op jit(solution)/shard_map/while/body/eval_jaxpr/hij,ihc->hjc/dot_general | solution.py:133
  270.9 0.8 copy.32
  271.7 1.7 fusion.28
  273.4 73.0 %reduce-scatter.5.cloned.1.call-done = f32[768,96]{0,1:T(8,128)} async-done(((f32[768,1536]{0,1:T(8,128)}), f32[768,96]{0,1:T(8,128)}) %reduce-scatter.5.cloned.1.call-update) | async-done | bytes 294928 | tf_op jit(solution)/shard_map/reduce_scatter | solution.py:94
  (37 shorter events, 0.9 us)
Async XLA Ops:
  7.2 4.7 %copy-start = (bf16[768,1536]{1,0:T(8,128)(2,1)S(1)}, bf16[768,1536]{1,0:T(8,128)(2,1)}, u32[]{:S(2)}) copy-start(bf16[768,1536]{1,0:T(8,128)(2,1)} %param.10) | copy-start | bytes 7077892
  7.2 6.3 %copy-start.6 = (bf16[1,128,768]{2,1,0:T(8,128)(2,1)S(1)}, bf16[1,128,768]{2,1,0:T(8,128)(2,1)}, u32[]{:S(2)}) copy-start(bf16[1,128,768]{2,1,0:T(8,128)(2,1)} %param.7) | copy-start | bytes 589828
  7.2 49.9 %all-gather.11.cloned.1.call-start = ((), (), s32[]{:S(2)}) async-start(), calls=%async_computation.5 | async-start | bytes 1769472 | tf_op jit(solution)/shard_map/all_gather | solution.py:75
  7.9 94.0 %all-gather.13.cloned.1.call-start = ((), (), s32[]{:S(2)}) async-start(), calls=%async_computation.6 | async-start | bytes 1769472 | tf_op jit(solution)/shard_map/all_gather | solution.py:76
  8.7 138.0 %all-gather.15.cloned.1.call-start = ((), (), s32[]{:S(2)}) async-start(), calls=%async_computation.7 | async-start | bytes 1769472 | tf_op jit(solution)/shard_map/all_gather | solution.py:142
  9.4 182.4 %all-gather.9.cloned.1.call-start = ((), (), s32[]{:S(2)}) async-start(), calls=%async_computation.3 | async-start | bytes 1769472 | tf_op jit(solution)/shard_map/all_gather | solution.py:143
  13.5 258.3 %reduce-scatter.3.cloned.1.call-start = ((), (), s32[]{:S(2)}) async-start(), calls=%async_computation.2 | async-start | bytes 589824 | tf_op jit(solution)/shard_map/reduce_scatter | solution.py:83
  14.3 93.6 %copy-start.8 = (pred[1024]{0:T(1024)(128)(4,1)}, pred[1024]{0:T(1024)(128)(4,1)S(1)}, u32[]{:S(2)}) copy-start(pred[1024]{0:T(1024)(128)(4,1)S(1)} %iota_compare_fusion) | copy-start | bytes 3076
  104.5 3.5 copy-start.3
  106.9 4.3 %copy-start.1 = (f32[8,128,1024]{2,1,0:T(8,128)}, f32[8,128,1024]{2,1,0:T(8,128)S(1)}, u32[]{:S(2)}) copy-start(f32[8,128,1024]{2,1,0:T(8,128)S(1)} %get-tuple-element.103) | copy-start | bytes 12582916
  112.5 233.9 %reduce-scatter.5.cloned.1.call-start = ((), (), s32[]{:S(2)}) async-start(), calls=%async_computation.4 | async-start | bytes 5013504 | tf_op jit(solution)/shard_map/reduce_scatter | solution.py:94
  115.5 0.9 copy-start.2
  115.5 1.1 copy-start.4
  115.5 1.3 copy-start.5
  149.3 110.9 %copy-start.9 = (pred[128]{0:T(512)(128)(4,1)S(1)}, pred[128]{0:T(512)(128)(4,1)}, u32[]{:S(2)}) copy-start(pred[128]{0:T(512)(128)(4,1)} %add_compare_fusion) | copy-start | bytes 388
  266.5 5.3 %copy-start.7 = (bf16[1,128,768]{2,1,0:T(8,128)(2,1)S(1)}, bf16[1,128,768]{2,1,0:T(8,128)(2,1)}, u32[]{:S(2)}) copy-start(bf16[1,128,768]{2,1,0:T(8,128)(2,1)} %param.11) | copy-start | bytes 589828
Sparse Core Ops, SparseCore 0:
  10.2 46.9 all-gather.10
  59.3 42.5 all-gather.12
  104.1 42.5 all-gather.14
  149.3 42.5 all-gather.8
  193.9 6.1 reduce-scatter.2
  205.7 140.5 reduce-scatter.4
where the time goes:
time: 354 us; the launch traced here: 353 us
  waiting for transfers between devices  225 us (64%)
  blocking collectives  63.9 us (18%)
  matrix products  30.9 us (9%)
  between operations  14.9 us (4%)
  local copies, waits for them, and re-layouts  14.5 us (4%)
    reduce_scatter x1, waiting for transfers between devices, shards(): lax.psum_scatter(weight_term, ('dp', 'seq'), scatter_dimension=1, tiled=T...  73 us
    all_gather x1, waiting for transfers between devices, shards(): lax.all_gather(own_k, 'seq', axis=0, tiled=True)  42.8 us
    all_gather x1, waiting for transfers between devices, shards(): lax.all_gather(grad_attn.astype(jnp.float32), 'seq', axis=0, tiled=True)  42.5 us
    all_gather x1, waiting for transfers between devices, shards(): lax.all_gather(own_v, 'seq', axis=0, tiled=True)  42.1 us
    all_gather x1, blocking collectives, shards(): lax.all_gather(log_sum.T, 'seq', axis=0, tiled=True)  30.8 us
    all_gather x1, blocking collectives, shards(): lax.all_gather(delta.T, 'seq', axis=0, tiled=True)  30.7 us
    all_gather x1, waiting for transfers between devices, shards(): lax.all_gather(own_q.astype(jnp.float32), 'seq', axis=0, tiled=True)  22.9 us
  transfers between devices with their start and end apart: 6, of which 5 were waited for; matrix products, arithmetic and copies ran while one was open for 14% of the time, Pallas kernels for 0%

commit v1 on v0

--- a/solution.py
+++ b/solution.py
@@ -68,14 +68,16 @@
         jnp.zeros((heads_here, frames_here), jnp.float32),
         jnp.zeros((heads_here, frames_here, HEAD_DIM), jnp.float32),
     )
-    run_max, run_sum, total = by_blocks(
-        forward_step,
-        start_state,
-        (
-            lax.all_gather(own_k, "seq", axis=0, tiled=True),
-            lax.all_gather(own_v, "seq", axis=0, tiled=True),
-        ),
-    )
+    grad_full = lax.all_gather(grad_out[0], "tensor", axis=1, tiled=True)
+    grad_attn = lax.dot_general(
+        grad_full, out_weight, (((1,), (1,)), ((), ())), preferred_element_type=jnp.float32
+    ).astype(jnp.bfloat16)
+    width = own_k.shape[1]
+    kv_all = lax.all_gather(jnp.concatenate([own_k, own_v], axis=1), "seq", axis=0, tiled=True)
+    qg_all = lax.all_gather(jnp.concatenate([own_q, grad_attn], axis=1), "seq", axis=0, tiled=True)
+    k_all = kv_all[:, :width]
+    v_all = kv_all[:, width:]
+    run_max, run_sum, total = by_blocks(forward_step, start_state, (k_all, v_all))
     log_sum = run_max + jnp.log(run_sum)
     attn_full = total / run_sum[:, :, None]
     attn = join_heads(attn_full).astype(jnp.bfloat16)
@@ -84,14 +86,12 @@
         partial_out.astype(jnp.bfloat16), "tensor", scatter_dimension=1, tiled=True
     ).astype(jnp.float32)
     block_out = (residual[0].astype(jnp.float32) + mixed).astype(jnp.bfloat16)
-    grad_full = lax.all_gather(grad_out[0], "tensor", axis=1, tiled=True)
-    grad_attn = lax.dot_general(
-        grad_full, out_weight, (((1,), (1,)), ((), ())), preferred_element_type=jnp.float32
-    ).astype(jnp.bfloat16)
     weight_term = lax.dot_general(
         attn, grad_full, (((0,), (0,)), ((), ())), preferred_element_type=jnp.float32
     )
-    grad_weight = lax.psum_scatter(weight_term, ("dp", "seq"), scatter_dimension=1, tiled=True)
+    grad_weight = lax.psum_scatter(
+        weight_term.astype(jnp.bfloat16), ("dp", "seq"), scatter_dimension=1, tiled=True
+    ).astype(jnp.float32)
     g_heads = split_heads(grad_attn)
     delta = jnp.sum(jnp.transpose(g_heads, (1, 0, 2)).astype(jnp.float32) * attn_full, axis=2)
 
@@ -109,14 +109,8 @@
         )
 
     empty_q = jnp.zeros((heads_here, frames_here, HEAD_DIM), jnp.float32)
-    grad_q = by_blocks(
-        query_step,
-        empty_q,
-        (
-            lax.all_gather(own_k, "seq", axis=0, tiled=True),
-            lax.all_gather(own_v, "seq", axis=0, tiled=True),
-        ),
-    )
+    grad_q = by_blocks(query_step, empty_q, (k_all, v_all))
+    stats = lax.all_gather(jnp.concatenate([log_sum, delta], axis=0), "seq", axis=1, tiled=True)
 
     def key_step(state, part, start):
         grad_k, grad_v = state
@@ -139,10 +133,10 @@
         key_step,
         (empty_q, empty_q),
         (
-            lax.all_gather(own_q.astype(jnp.float32), "seq", axis=0, tiled=True),
-            lax.all_gather(grad_attn.astype(jnp.float32), "seq", axis=0, tiled=True),
-            lax.all_gather(log_sum.T, "seq", axis=0, tiled=True),
-            lax.all_gather(delta.T, "seq", axis=0, tiled=True),
+            qg_all[:, :width],
+            qg_all[:, width:],
+            stats[:heads_here].T,
+            stats[heads_here:].T,
         ),
     )
     return (

time: 354 us -> 286 us (0.81)
  waiting for transfers between devices: 225 us -> 178 us
  blocking collectives: 63.9 us -> 33.1 us
  local copies, waits for them, and re-layouts: 14.5 us -> 21.1 us
  other arithmetic: 3.3 us -> 8.09 us
    all_gather x4 -> x2, waiting for transfers between devices: 150 us -> 91.4 us  [the longest x1 58.7 us: shards(): lax.all_gather(jnp.concatenate([own_k, own_v], axis=1), 'seq', axis=0, ti...]
    all_gather x2 -> x1, blocking collectives: 61.5 us -> 30.7 us  [shards(): lax.all_gather(jnp.concatenate([log_sum, delta], axis=0), 'seq', axis=1,...]
    slice x0 -> x7, local copies, waits for them, and re-layouts: none -> 17.9 us  [the longest x2 6.4 us: shards(): k_all = kv_all[:, :width]]
    reduce_scatter x1, waiting for transfers between devices: 73 us -> 86.8 us  [shards(): lax.psum_scatter(weight_term.astype(jnp.bfloat16), ('dp', 'seq'), scatter...]
    all_gather x2 -> x0, local copies, waits for them, and re-layouts: 5.23 us -> none  [the longest x1 2.64 us: shards(): lax.all_gather(own_k, 'seq', axis=0, tiled=True)]
    convert_element_type x2 -> x0, local copies, waits for them, and re-layouts: 5.22 us -> none  [the longest x1 2.64 us: key_step(): q_part = split_heads(q_rows.astype(jnp.bfloat16))]
  transfers between devices with their start and end apart: 6 -> 4, of which waited for: 5 -> 3; matrix products, arithmetic and copies ran while one was open for 14% -> 20% of each run, Pallas kernels for 0% -> 0%
where the time goes in v1:
time: 286 us
  waiting for transfers between devices  178 us (62%)
  blocking collectives  33.1 us (12%)
  matrix products  30.6 us (11%)
  local copies, waits for them, and re-layouts  21.1 us (7%)
  between operations  14.6 us (5%)
  other arithmetic  8.09 us (3%)
    reduce_scatter x1, waiting for transfers between devices, shards(): lax.psum_scatter(weight_term.astype(jnp.bfloat16), ('dp', 'seq'), scatter...  86.8 us
    all_gather x1, waiting for transfers between devices, shards(): lax.all_gather(jnp.concatenate([own_k, own_v], axis=1), 'seq', axis=0, ti...  58.7 us
    all_gather x1, waiting for transfers between devices, shards(): lax.all_gather(jnp.concatenate([own_q, grad_attn], axis=1), 'seq', axis=0...  32.7 us
    all_gather x1, blocking collectives, shards(): lax.all_gather(jnp.concatenate([log_sum, delta], axis=0), 'seq', axis=1,...  30.7 us
    dot_general x2, matrix products, masked_scores(): jnp.einsum('ihc,jhc->hij', left, right, preferred_element_type=jnp.float32)  7.05 us
    slice x2, local copies, waits for them, and re-layouts, shards(): k_all = kv_all[:, :width]  6.4 us
    slice x2, local copies, waits for them, and re-layouts, shards(): qg_all[:, width:]  6.32 us
    dot_general x1, matrix products, key_step(): jnp.einsum('hij,ihc->hjc', dscores, q_part, preferred_element_type=jnp.fl...  6.25 us
  transfers between devices with their start and end apart: 4, of which 3 were waited for; matrix products, arithmetic and copies ran while one was open for 20% of the time, Pallas kernels for 0%

profile of v1, /device:TPU:0, one launch (start us, length us, event | category | flops | bytes accessed | tf_op | source)
XLA Modules:
  0.0 285.8 jit_solution(12319059477176468410)
XLA Ops:
  7.2 2.0 pad_maximum_fusion
  9.3 2.4 all-gather
  11.7 0.9 convolution_convert_fusion.2
  12.6 0.8 pad_maximum_fusion.1
  13.4 0.2 copy.26
  14.3 58.7 %all-gather.4.cloned.1.call-done = bf16[1024,1536]{1,0:T(8,128)(2,1)} async-done(((bf16[128,1536]{1,0:T(8,128)(2,1)}), bf16[1024,1536]{1,0:T(8,128)(2,1)}) %all-gather.4.cloned.1.call-update) | async-done | bytes 3145744 | tf_op jit(solution)/shard_map/all_gather | solution.py:76
  73.0 3.8 %fusion.44 = (bf16[1024,768]{1,0:T(8,128)(2,1)}, bf16[1024,768]{1,0:T(8,128)(2,1)}) fusion(bf16[1024,1536]{1,0:T(8,128)(2,1)} %all-gather.4.cloned.1.call-done), kind=kLoop, calls=%fused_computation.61 | loop fusion | bytes 6291456 | tf_op jit(solution)/shard_map/slice | solution.py:78
  76.8 2.6 copy.25
  79.4 2.6 copy.27
  81.9 2.9 %bitcast_reduce_fusion = (f32[8,128]{1,0:T(8,128)S(1)}, f32[8,1024,128]{2,1,0:T(8,128)S(1)}) fusion(pred[1024]{0:T(1024)(128)(4,1)S(1)} %iota_compare_fusion, bf16[1024,8,96]{0,2,1:T(8,128)(2,1)} %bitcast.88, bf16[128,8,96]{0,2,1:T(8,128)(2,1)S(1)} %bitcast.97), kind=kOutput, calls=%fused_computation.2 | convolution fusion | flops 204471296 | bytes 5968896 | tf_op jit(solution)/shard_map/while/body/eval_jaxpr/ihc,jhc->hij/dot_general | solution.py:49
  84.8 0.9 fusion.5
  85.8 3.6 %fusion.31 = (bf16[128,8,96]{0,2,1:T(8,128)(2,1)S(1)}, f32[8,128,96]{1,2,0:T(8,128)}) fusion(f32[128,8]{0,1:T(8,128)S(1)} %bitcast_add_fusion.1, f32[128,8]{0,1:T(8,128)S(1)} %get-tuple-element.104, bf16[1024,8,96]{0,2,1:T(8,128)(2,1)S(1)} %bitcast.93, f32[8,1024,128]{2,1,0:T(8,128)S(1)} %get-tuple-element.107, f32[8,128]{1,0:T(8,128)S(1)} %broadcast_maximum_fusion, ...), kind=kOutput, calls=%fused_computation.41 | convolution fusion | flops 1211400192 | bytes 6370304 | tf_op jit(solution)/shard_map/while/body/eval_jaxpr/hij,jhc->hic/dot_general | solution.py:61
  89.4 1.3 convolution_convert_fusion.1
  90.7 2.3 convolution_convert_fusion
  93.1 0.2 copy.29
  93.4 0.2 copy.34
  93.6 1.1 fusion.27
  94.7 5.6 %fusion.21 = bf16[8,128,96]{1,2,0:T(8,128)(2,1)S(1)} fusion(bf16[1024,8,96]{0,2,1:T(8,128)(2,1)} %bitcast.89, f32[8,1024,128]{2,1,0:T(8,128)} %copy-done.1, bf16[128,8,96]{0,2,1:T(8,128)(2,1)S(1)} %bitcast.104, bf16[1024,8,96]{0,2,1:T(8,128)(2,1)} %bitcast.92, f32[8,128]{1,0:T(8,128)S(1)} %fusion.27, f32[8,128]{1,0:T(8,128)S(1)} %get-tuple-element.102, ...), kind=kOutput, calls=%fused_computation.27 | convolution fusion | flops 410091520 | bytes 7742464 | tf_op jit(solution)/shard_map/while/body/eval_jaxpr/hij,jhc->hic/dot_general | solution.py:107
  100.3 0.8 copy.35
  101.1 32.7 %all-gather.6.cloned.1.call-done = bf16[1024,1536]{1,0:T(8,128)(2,1)} async-done(((bf16[128,1536]{1,0:T(8,128)(2,1)}), bf16[1024,1536]{1,0:T(8,128)(2,1)}) %all-gather.6.cloned.1.call-update) | async-done | bytes 3145744 | tf_op jit(solution)/shard_map/all_gather | solution.py:77
  133.9 3.7 %fusion.43 = (bf16[1024,768]{1,0:T(8,128)(2,1)}, bf16[1024,768]{1,0:T(8,128)(2,1)}) fusion(bf16[1024,1536]{1,0:T(8,128)(2,1)} %all-gather.6.cloned.1.call-done), kind=kLoop, calls=%fused_computation.60 | loop fusion | bytes 6291456 | tf_op jit(solution)/shard_map/slice | solution.py:137
  137.6 2.6 copy.31
  140.2 2.6 copy.33
  142.8 30.7 %all_gather.15 = f32[16,1024]{1,0:T(8,128)S(1)} all-gather(f32[16,128]{1,0:T(8,128)S(1)} %pad_maximum_fusion.2), channel_id=1, replica_groups=mesh['dp'=2,'seq'=8,'tensor'=2] {'seq'}, dimensions={1}, use_global_device_ids=true | all-gather | bytes 73728 | tf_op jit(solution)/shard_map/all_gather | solution.py:113
  173.5 4.2 %fusion.46 = f32[8,1024,128]{2,1,0:T(8,128)} fusion(bf16[1024,8,96]{0,2,1:T(8,128)(2,1)} %bitcast.90, bf16[128,8,96]{0,2,1:T(8,128)(2,1)S(1)} %bitcast.96), kind=kOutput, calls=%fused_computation.63 | convolution fusion | flops 201326592 | bytes 5963776 | tf_op jit(solution)/shard_map/while/body/eval_jaxpr/ihc,jhc->hij/dot_general | solution.py:49
  177.7 6.2 %fusion.22 = bf16[8,128,96]{1,2,0:T(8,128)(2,1)S(1)} fusion(bf16[1024,8,96]{0,2,1:T(8,128)(2,1)} %bitcast.91, f32[8,1024,128]{2,1,0:T(8,128)} %fusion.46, bf16[1024,8,96]{0,2,1:T(8,128)(2,1)} %bitcast.94, bf16[128,8,96]{0,2,1:T(8,128)(2,1)S(1)} %bitcast.105, f32[8,1024]{1,0:T(8,128)S(1)} %get-tuple-element.101, f32[8,1024]{1,0:T(8,128)S(1)} %get-tuple-element.100, ...), kind=kOutput, calls=%fused_computation.28 | convolution fusion | flops 410091520 | bytes 7798912 | tf_op jit(solution)/shard_map/while/body/eval_jaxpr/hij,ihc->hjc/dot_general | solution.py:124
  184.0 0.8 copy.36
  184.8 3.6 %fusion.23 = bf16[8,128,96]{1,2,0:T(8,128)(2,1)S(1)} fusion(bf16[1024,8,96]{0,2,1:T(8,128)(2,1)} %bitcast.95, f32[8,1024,128]{2,1,0:T(8,128)} %fusion.46, f32[8,1024]{1,0:T(8,128)S(1)} %get-tuple-element.100, pred[128]{0:T(512)(128)(4,1)S(1)} %add_compare_fusion), kind=kOutput, calls=%fused_computation.29 | convolution fusion | flops 205619200 | bytes 5996672 | tf_op jit(solution)/shard_map/while/body/eval_jaxpr/hij,ihc->hjc/dot_general | solution.py:127
  188.4 0.8 copy.37
  189.2 1.7 fusion.32
  190.9 86.8 %reduce-scatter.5.cloned.1.call-done = bf16[768,96]{0,1:T(8,128)(2,1)} async-done(((bf16[768,1536]{0,1:T(8,128)(2,1)}), bf16[768,96]{0,1:T(8,128)(2,1)}) %reduce-scatter.5.cloned.1.call-update) | async-done | bytes 147472 | tf_op jit(solution)/shard_map/reduce_scatter | solution.py:92
  277.6 1.6 convert_element_type.121
  (31 shorter events, 0.5 us)
Async XLA Ops:
  7.2 4.5 %copy-start = (bf16[768,1536]{1,0:T(8,128)(2,1)S(1)}, bf16[768,1536]{1,0:T(8,128)(2,1)}, u32[]{:S(2)}) copy-start(bf16[768,1536]{1,0:T(8,128)(2,1)} %param.10) | copy-start | bytes 7077892
  7.2 5.4 %copy-start.3 = (bf16[1,128,768]{2,1,0:T(8,128)(2,1)S(1)}, bf16[1,128,768]{2,1,0:T(8,128)(2,1)}, u32[]{:S(2)}) copy-start(bf16[1,128,768]{2,1,0:T(8,128)(2,1)} %param.7) | copy-start | bytes 589828
  7.2 65.8 %all-gather.4.cloned.1.call-start = ((), (), s32[]{:S(2)}) async-start(), calls=%async_computation.2 | async-start | bytes 3538944 | tf_op jit(solution)/shard_map/all_gather | solution.py:76
  9.2 124.6 %all-gather.6.cloned.1.call-start = ((), (), s32[]{:S(2)}) async-start(), calls=%async_computation.4 | async-start | bytes 3538944 | tf_op jit(solution)/shard_map/all_gather | solution.py:77
  13.4 175.8 %reduce-scatter.3.cloned.1.call-start = ((), (), s32[]{:S(2)}) async-start(), calls=%async_computation.3 | async-start | bytes 589824 | tf_op jit(solution)/shard_map/reduce_scatter | solution.py:85
  81.9 3.9 %copy-start.2 = (bf16[1024,768]{0,1:T(8,128)(2,1)S(1)}, bf16[1024,768]{0,1:T(8,128)(2,1)}, u32[]{:S(2)}) copy-start(bf16[1024,768]{0,1:T(8,128)(2,1)} %copy.27) | copy-start | bytes 4718596
  84.8 4.6 %copy-start.1 = (f32[8,1024,128]{2,1,0:T(8,128)}, f32[8,1024,128]{2,1,0:T(8,128)S(1)}, u32[]{:S(2)}) copy-start(f32[8,1024,128]{2,1,0:T(8,128)S(1)} %get-tuple-element.107) | copy-start | bytes 12582916
  89.4 3.9 %copy-start.4 = (bf16[1,128,768]{2,1,0:T(8,128)(2,1)S(1)}, bf16[1,128,768]{2,1,0:T(8,128)(2,1)}, u32[]{:S(2)}) copy-start(bf16[1,128,768]{2,1,0:T(8,128)(2,1)} %param.8) | copy-start | bytes 589828
  89.4 4.0 %copy-start.5 = (bf16[1,128,768]{2,1,0:T(8,128)(2,1)S(1)}, bf16[1,128,768]{2,1,0:T(8,128)(2,1)}, u32[]{:S(2)}) copy-start(bf16[1,128,768]{2,1,0:T(8,128)(2,1)} %param.9) | copy-start | bytes 589828
  90.7 186.9 %reduce-scatter.5.cloned.1.call-start = ((), (), s32[]{:S(2)}) async-start(), calls=%async_computation.5 | async-start | bytes 2506752 | tf_op jit(solution)/shard_map/reduce_scatter | solution.py:92
  183.9 5.3 %copy-start.6 = (bf16[1,128,768]{2,1,0:T(8,128)(2,1)S(1)}, bf16[1,128,768]{2,1,0:T(8,128)(2,1)}, u32[]{:S(2)}) copy-start(bf16[1,128,768]{2,1,0:T(8,128)(2,1)} %param.11) | copy-start | bytes 589828
Sparse Core Ops, SparseCore 0:
  10.2 62.7 all-gather.3
  75.1 58.6 all-gather.5
  136.1 6.4 reduce-scatter.2
  147.4 130.1 reduce-scatter.4

commit v2 on v1

v2 whole, which is shorter than its diff:
```python
import math

import jax
import jax.numpy as jnp
from jax import lax
from jax.sharding import PartitionSpec as P

HEAD_DIM = 96


def split_heads(rows):
    return rows.reshape(rows.shape[0], -1, HEAD_DIM)


def join_heads(blocks):
    return jnp.transpose(blocks, (1, 0, 2)).reshape(blocks.shape[1], -1)


def shifted_blocks(x, axis_name, n):
    blocks = [x]
    for k in range(1, n):
        perm = [(i, (i + k) % n) for i in range(n)]
        blocks.append(lax.ppermute(x, axis_name, perm))
    return blocks


def shards(queries, keys, values, out_weight, residual, lengths, grad_out):
    scale = 1.0 / math.sqrt(HEAD_DIM)
    highest = lax.Precision.HIGHEST
    n_seq = lax.axis_size("seq")
    n_dp = lax.axis_size("dp")
    me = lax.axis_index("seq")
    own_q = queries[0]
    own_k = keys[0]
    own_v = values[0]
    frames_here = own_q.shape[0]
    width = own_q.shape[1]
    length = lengths[0]
    q_heads = split_heads(own_q)
    k_heads = split_heads(own_k)
    v_heads = split_heads(own_v)
    heads_here = q_heads.shape[1]
    frame_ids = jnp.arange(frames_here, dtype=jnp.int32)
    key_pos = me * frames_here + frame_ids

    def source_of(k):
        return (me - k + n_seq) % n_seq

    def masked_scores(left, right, positions):
        s = jnp.einsum("ihc,jhc->hij", left, right, preferred_element_type=jnp.float32) * scale
        return jnp.where(positions[None, None, :] < length, s, -1e30)

    grad_full = lax.all_gather(grad_out[0], "tensor", axis=1, tiled=True)
    grad_attn = lax.dot_general(
        grad_full, out_weight, (((1,), (1,)), ((), ())), preferred_element_type=jnp.float32
    ).astype(jnp.bfloat16)
    g_heads = split_heads(grad_attn)

    kv_blocks = shifted_blocks(jnp.concatenate([own_k, own_v], axis=1), "seq", n_seq)
    qg_blocks = shifted_blocks(jnp.concatenate([own_q, grad_attn], axis=1), "seq", n_seq)

    run_max = jnp.full((heads_here, frames_here), -1e30, jnp.float32)
    run_sum = jnp.zeros((heads_here, frames_here), jnp.float32)
    total = jnp.zeros((heads_here, frames_here, HEAD_DIM), jnp.float32)
    for k, kv in enumerate(kv_blocks):
        positions = source_of(k) * frames_here + frame_ids
        s = masked_scores(q_heads, split_heads(kv[:, :width]), positions)
        new_max = jnp.maximum(run_max, jnp.max(s, axis=2))
        factor = jnp.exp(run_max - new_max)
        weights = jnp.exp(s - new_max[:, :, None])
        run_sum = run_sum * factor + jnp.sum(weights, axis=2)
        total = total * factor[:, :, None] + jnp.einsum(
            "hij,jhc->hic", weights, split_heads(kv[:, width:]).astype(jnp.float32), precision=highest
        )
        run_max = new_max
    log_sum = run_max + jnp.log(run_sum)
    attn_full = total / run_sum[:, :, None]
    attn = join_heads(attn_full).astype(jnp.bfloat16)
    partial_out = jnp.dot(attn, out_weight, preferred_element_type=jnp.float32)
    mixed = lax.psum_scatter(
        partial_out.astype(jnp.bfloat16), "tensor", scatter_dimension=1, tiled=True
    ).astype(jnp.float32)
    block_out = (residual[0].astype(jnp.float32) + mixed).astype(jnp.bfloat16)

    delta = jnp.sum(jnp.transpose(g_heads, (1, 0, 2)).astype(jnp.float32) * attn_full, axis=2)
    stat_blocks = shifted_blocks(jnp.concatenate([log_sum, delta], axis=0), "seq", n_seq)

    col_width = grad_full.shape[1] // (n_dp * n_seq)
    g_cols = grad_full.reshape(frames_here, n_dp, n_seq, col_width)
    ag_blocks = []
    for k in range(n_seq):
        target = (me + k) % n_seq
        cols = lax.dynamic_index_in_dim(g_cols, target, axis=2, keepdims=False)
        piece = jnp.concatenate([attn, cols.reshape(frames_here, n_dp * col_width)], axis=1)
        if k == 0:
            ag_blocks.append(piece)
        else:
            perm = [(i, (i + k) % n_seq) for i in range(n_seq)]
            ag_blocks.append(lax.ppermute(piece, "seq", perm))
    weight_term = jnp.zeros((width, n_dp * col_width), jnp.float32)
    for piece in ag_blocks:
        weight_term = weight_term + lax.dot_general(
            piece[:, :width], piece[:, width:], (((0,), (0,)), ((), ())),
            preferred_element_type=jnp.float32,
        )
    grad_weight = lax.psum_scatter(weight_term, "dp", scatter_dimension=1, tiled=True)

    grad_q = jnp.zeros((heads_here, frames_here, HEAD_DIM), jnp.float32)
    for k, kv in enumerate(kv_blocks):
        positions = source_of(k) * frames_here + frame_ids
        k_rows = split_heads(kv[:, :width])
        s = masked_scores(q_heads, k_rows, positions)
        probs = jnp.exp(s - log_sum[:, :, None])
        dots = jnp.einsum(
            "ihc,jhc->hij", g_heads, split_heads(kv[:, width:]), preferred_element_type=jnp.float32
        )
        dscores = (probs * (dots - delta[:, :, None]) * scale).astype(jnp.bfloat16)
        grad_q = grad_q + jnp.einsum("hij,jhc->hic", dscores, k_rows, preferred_element_type=jnp.float32)

    grad_k = jnp.zeros((heads_here, frames_here, HEAD_DIM), jnp.float32)
    grad_v = jnp.zeros((heads_here, frames_here, HEAD_DIM), jnp.float32)
    for qg, stats in zip(qg_blocks, stat_blocks):
        q_part = split_heads(qg[:, :width])
        g_part = split_heads(qg[:, width:])
        s = masked_scores(q_part, k_heads, key_pos)
        probs = jnp.exp(s - stats[:heads_here][:, :, None])
        dots = jnp.einsum("ihc,jhc->hij", g_part, v_heads, preferred_element_type=jnp.float32)
        dscores = (probs * (dots - stats[heads_here:][:, :, None]) * scale).astype(jnp.bfloat16)
        grad_k = grad_k + jnp.einsum("hij,ihc->hjc", dscores, q_part, preferred_element_type=jnp.float32)
        grad_v = grad_v + jnp.einsum(
            "hij,ihc->hjc", probs.astype(jnp.bfloat16), g_part, preferred_element_type=jnp.float32
        )
    return (
        block_out[None],
        join_heads(grad_q).astype(jnp.bfloat16)[None],
        join_heads(grad_k).astype(jnp.bfloat16)[None],
        join_heads(grad_v).astype(jnp.bfloat16)[None],
        grad_weight,
    )


def solution(mesh):
    in_specs = (
        P("dp", "seq", "tensor"),
        P("dp", "seq", "tensor"),
        P("dp", "seq", "tensor"),
        P("tensor", None),
        P("dp", "seq", "tensor"),
        P("dp"),
        P("dp", "seq", "tensor"),
    )
    out_specs = (
        P("dp", "seq", "tensor"),
        P("dp", "seq", "tensor"),
        P("dp", "seq", "tensor"),
        P("dp", "seq", "tensor"),
        P("tensor", ("dp", "seq")),
    )
    return jax.shard_map(shards, mesh=mesh, in_specs=in_specs, out_specs=out_specs, check_vma=False)
```

time: 286 us -> 343 us (1.20)
  waiting for transfers between devices: 178 us -> 32.8 us
  starting transfers between devices: 0.16 us -> 83.7 us
  matrix products: 30.6 us -> 105 us
  local copies, waits for them, and re-layouts: 21.1 us -> 74 us
  blocking collectives: 33.1 us -> 2.09 us
  other arithmetic: 8.09 us -> 27.7 us
    all_gather x2 -> x0, waiting for transfers between devices: 91.4 us -> none  [the longest x1 58.7 us: shards(): lax.all_gather(jnp.concatenate([own_k, own_v], axis=1), 'seq', axis=0, ti...]
    ppermute x0 -> x28, starting transfers between devices: none -> 83.4 us  [the longest x21 72 us: shifted_blocks(): blocks.append(lax.ppermute(x, axis_name, perm))]
    reduce_scatter x1, waiting for transfers between devices: 86.8 us -> 5.01 us  [shards(): lax.psum_scatter(weight_term, 'dp', scatter_dimension=1, tiled=True)]
    dot_general x5 -> x41, matrix products: 21.4 us -> 82.5 us  [the longest x8 20.6 us: shards(): jnp.einsum('hij,jhc->hic', dscores, k_rows, preferred_element_type=jnp.fl...]
    slice x7 -> x49, local copies, waits for them, and re-layouts: 17.9 us -> 60.9 us  [the longest x13 21 us: shards(): kv[:, width:]]
    all_gather x1 -> x0, blocking collectives: 30.7 us -> none  [shards(): lax.all_gather(jnp.concatenate([log_sum, delta], axis=0), 'seq', axis=1,...]
    ppermute x0 -> x28, waiting for transfers between devices: none -> 27.8 us  [the longest x21 18.4 us: shifted_blocks(): blocks.append(lax.ppermute(x, axis_name, perm))]
    dot_general x2 -> x15, matrix products: 7.05 us -> 20.2 us  [masked_scores(): jnp.einsum('ihc,jhc->hij', left, right, preferred_element_type=jnp.float32)]
  transfers between devices with their start and end apart: 4 -> 30, of which waited for: 3 -> 4; matrix products, arithmetic and copies ran while one was open for 20% -> 60% of each run, Pallas kernels for 0% -> 0%
where the time goes in v2:
time: 343 us; the launch traced here: 340 us
  matrix products  105 us (31%)
  starting transfers between devices  83.7 us (24%)
  local copies, waits for them, and re-layouts  74 us (22%)
  waiting for transfers between devices  32.8 us (10%)
  other arithmetic  27.7 us (8%)
  between operations  15.5 us (5%)
    ppermute x21, starting transfers between devices, shifted_blocks(): blocks.append(lax.ppermute(x, axis_name, perm))  72 us
    slice x13, local copies, waits for them, and re-layouts, shards(): kv[:, width:]  21 us
    slice x14, local copies, waits for them, and re-layouts, shards(): g_part = split_heads(qg[:, width:])  20.6 us
    dot_general x8, matrix products, shards(): jnp.einsum('hij,jhc->hic', dscores, k_rows, preferred_element_type=jnp.fl...  20.6 us
    dot_general x15, matrix products, masked_scores(): jnp.einsum('ihc,jhc->hij', left, right, preferred_element_type=jnp.float32)  20.2 us
    dot_general x8, matrix products, shards(): jnp.einsum('hij,jhc->hic', weights, split_heads(kv[:, width:]).astype(jnp...  19.4 us
    ppermute x21, waiting for transfers between devices, shifted_blocks(): blocks.append(lax.ppermute(x, axis_name, perm))  18.4 us
    dot_general x8, matrix products, shards(): jnp.einsum('hij,ihc->hjc', dscores, q_part, preferred_element_type=jnp.fl...  18.2 us
  transfers between devices with their start and end apart: 30, of which 4 were waited for; matrix products, arithmetic and copies ran while one was open for 60% of the time, Pallas kernels for 0%

profile of v2, /device:TPU:0, one launch (start us, length us, event | category | flops | bytes accessed | tf_op | source)
XLA Modules:
  0.0 340.5 jit_solution(1692935442407498465)
XLA Ops:
  9.2 5.1 %collective-permute-start.5 = (bf16[128,1536]{1,0:T(8,128)(2,1)}, bf16[128,1536]{1,0:T(8,128)(2,1)}, u32[]{:S(2)}, u32[]{:S(2)}) collective-permute-start(bf16[128,1536]{1,0:T(8,128)(2,1)} %pad_maximum_fusion), channel_id=1, source_target_pairs={{0,12},{2,14},{4,0},{6,2},{8,4},{10,6},{12,8},{14,10},{1,13},{3,15... | collective-permute-start | bytes 1179656 | tf_op jit(solution)/shard_map/ppermute | solution.py:23
  15.7 3.0 collective-permute-start.3
  43.5 18.6 %collective-permute-start.19 = (bf16[128,1536]{1,0:T(8,128)(2,1)}, bf16[128,1536]{1,0:T(8,128)(2,1)}, u32[]{:S(2)}, u32[]{:S(2)}) collective-permute-start(bf16[128,1536]{1,0:T(8,128)(2,1)} %pad_maximum_fusion.1), channel_id=1, source_target_pairs={{0,14},{2,0},{4,2},{6,4},{8,6},{10,8},{12,10},{14,12},{1,15},{3,1}... | collective-permute-start | bytes 1179656 | tf_op jit(solution)/shard_map/ppermute | solution.py:23
  64.6 18.4 %collective-permute-done.3 = bf16[128,1536]{1,0:T(8,128)(2,1)} collective-permute-done((bf16[128,1536]{1,0:T(8,128)(2,1)}, bf16[128,1536]{1,0:T(8,128)(2,1)}, u32[]{:S(2)}, u32[]{:S(2)}) %collective-permute-start.3) | collective-permute-done | bytes 393248 | tf_op jit(solution)/shard_map/ppermute | solution.py:23
  85.6 9.3 %collective-permute-start.15 = (bf16[128,1536]{1,0:T(8,128)(2,1)}, bf16[128,1536]{1,0:T(8,128)(2,1)}, u32[]{:S(2)}, u32[]{:S(2)}) collective-permute-start(bf16[128,1536]{1,0:T(8,128)(2,1)} %pad_maximum_fusion.1), channel_id=1, source_target_pairs={{0,10},{2,12},{4,14},{6,0},{8,2},{10,4},{12,6},{14,8},{1,11},{3,13... | collective-permute-start | bytes 1179656 | tf_op jit(solution)/shard_map/ppermute | solution.py:23
  99.3 10.6 %collective-permute-start.11 = (bf16[128,1536]{1,0:T(8,128)(2,1)}, bf16[128,1536]{1,0:T(8,128)(2,1)}, u32[]{:S(2)}, u32[]{:S(2)}) collective-permute-start(bf16[128,1536]{1,0:T(8,128)(2,1)} %pad_maximum_fusion.1), channel_id=1, source_target_pairs={{0,6},{2,8},{4,10},{6,12},{8,14},{10,0},{12,2},{14,4},{1,7},{3,9},... | collective-permute-start | bytes 1179656 | tf_op jit(solution)/shard_map/ppermute | solution.py:23
  130.2 2.6 fusion.135
  136.5 2.6 fusion.133
  142.9 2.6 fusion.131
  149.3 2.6 fusion.129
  153.6 2.7 fusion.127
  156.3 2.4 fusion.124
  165.9 3.4 fusion.146
  169.8 2.6 fusion.105
  172.4 2.5 fusion.106
  181.7 2.5 fusion.107
  184.2 10.8 %collective-permute-start.7 = (bf16[128,1536]{1,0:T(8,128)(2,1)}, bf16[128,1536]{1,0:T(8,128)(2,1)}, u32[]{:S(2)}, u32[]{:S(2)}) collective-permute-start(bf16[128,1536]{1,0:T(8,128)(2,1)} %pad_maximum_fusion.1), channel_id=1, source_target_pairs={{0,2},{2,4},{4,6},{6,8},{8,10},{10,12},{12,14},{14,0},{1,3},{3,5},... | collective-permute-start | bytes 1179656 | tf_op jit(solution)/shard_map/ppermute | solution.py:23
  196.8 2.5 fusion.108
  203.7 2.5 fusion.109
  206.3 3.4 collective-permute-start.20
  219.2 2.6 convolution_add_fusion.7
  221.8 4.3 %collective-permute-start.14 = (f32[16,128]{1,0:T(8,128)}, f32[16,128]{1,0:T(8,128)}, u32[]{:S(2)}, u32[]{:S(2)}) collective-permute-start(f32[16,128]{1,0:T(8,128)} %pad_maximum_fusion.9), channel_id=1, source_target_pairs={{0,8},{2,10},{4,12},{6,14},{8,0},{10,2},{12,4},{14,6},{1,9},{3,11}... | collective-permute-start | bytes 24584 | tf_op jit(solution)/shard_map/ppermute | solution.py:23
  227.9 3.0 fusion.99
  267.8 3.3 collective-permute-start.27
  284.1 2.4 fusion.102
  288.8 2.4 fusion.104
  291.2 2.5 convolution_add_fusion.5
  293.7 2.9 fusion.98
  298.8 3.1 collective-permute-start.23
  306.9 6.2 %collective-permute-done.24 = bf16[128,960]{0,1:T(8,128)(2,1)} collective-permute-done((bf16[128,960]{0,1:T(8,128)(2,1)}, bf16[128,960]{0,1:T(8,128)(2,1)}, u32[]{:S(2)}, u32[]{:S(2)}) %collective-permute-start.24) | collective-permute-done | bytes 245792 | tf_op jit(solution)/shard_map/ppermute | solution.py:99
  314.3 3.1 collective-permute-done.23
  328.6 5.0 %reduce-scatter.5.cloned.1.call-done = f32[768,96]{0,1:T(8,128)} async-done(((f32[768,192]{0,1:T(8,128)}), f32[768,96]{0,1:T(8,128)}) %reduce-scatter.5.cloned.1.call-update) | async-done | bytes 294928 | tf_op jit(solution)/shard_map/reduce_scatter | solution.py:106
  (288 shorter events, 173.7 us)
Async XLA Ops:
  7.2 319.8 %reduce-scatter.3.cloned.1.call-start = ((), (), s32[]{:S(2)}) async-start(), calls=%async_computation.2 | async-start | bytes 589824 | tf_op jit(solution)/shard_map/reduce_scatter | solution.py:80
  9.2 26.0 %collective-permute-start.5 = (bf16[128,1536]{1,0:T(8,128)(2,1)}, bf16[128,1536]{1,0:T(8,128)(2,1)}, u32[]{:S(2)}, u32[]{:S(2)}) collective-permute-start(bf16[128,1536]{1,0:T(8,128)(2,1)} %pad_maximum_fusion), channel_id=1, source_target_pairs={{0,12},{2,14},{4,0},{6,2},{8,4},{10,6},{12,8},{14,10},{1,13},{3,15... | collective-permute-start | bytes 1179656 | tf_op jit(solution)/shard_map/ppermute | solution.py:23
  14.3 25.2 %collective-permute-start.6 = (bf16[128,1536]{1,0:T(8,128)(2,1)}, bf16[128,1536]{1,0:T(8,128)(2,1)}, u32[]{:S(2)}, u32[]{:S(2)}) collective-permute-start(bf16[128,1536]{1,0:T(8,128)(2,1)} %pad_maximum_fusion), channel_id=1, source_target_pairs={{0,14},{2,0},{4,2},{6,4},{8,6},{10,8},{12,10},{14,12},{1,15},{3,1}... | collective-permute-start | bytes 1179656 | tf_op jit(solution)/shard_map/ppermute | solution.py:23
  15.7 27.8 %collective-permute-start.4 = (bf16[128,1536]{1,0:T(8,128)(2,1)}, bf16[128,1536]{1,0:T(8,128)(2,1)}, u32[]{:S(2)}, u32[]{:S(2)}) collective-permute-start(bf16[128,1536]{1,0:T(8,128)(2,1)} %pad_maximum_fusion), channel_id=1, source_target_pairs={{0,10},{2,12},{4,14},{6,0},{8,2},{10,4},{12,6},{14,8},{1,11},{3,13... | collective-permute-start | bytes 1179656 | tf_op jit(solution)/shard_map/ppermute | solution.py:23
  15.7 67.3 %collective-permute-start.3 = (bf16[128,1536]{1,0:T(8,128)(2,1)}, bf16[128,1536]{1,0:T(8,128)(2,1)}, u32[]{:S(2)}, u32[]{:S(2)}) collective-permute-start(bf16[128,1536]{1,0:T(8,128)(2,1)} %pad_maximum_fusion), channel_id=1, source_target_pairs={{0,8},{2,10},{4,12},{6,14},{8,0},{10,2},{12,4},{14,6},{1,9},{3,11}... | collective-permute-start | bytes 1179656 | tf_op jit(solution)/shard_map/ppermute | solution.py:23
  18.7 66.9 %collective-permute-start.2 = (bf16[128,1536]{1,0:T(8,128)(2,1)}, bf16[128,1536]{1,0:T(8,128)(2,1)}, u32[]{:S(2)}, u32[]{:S(2)}) collective-permute-start(bf16[128,1536]{1,0:T(8,128)(2,1)} %pad_maximum_fusion), channel_id=1, source_target_pairs={{0,6},{2,8},{4,10},{6,12},{8,14},{10,0},{12,2},{14,4},{1,7},{3,9},... | collective-permute-start | bytes 1179656 | tf_op jit(solution)/shard_map/ppermute | solution.py:23
  35.2 62.2 %collective-permute-start = (bf16[128,1536]{1,0:T(8,128)(2,1)}, bf16[128,1536]{1,0:T(8,128)(2,1)}, u32[]{:S(2)}, u32[]{:S(2)}) collective-permute-start(bf16[128,1536]{1,0:T(8,128)(2,1)} %pad_maximum_fusion), channel_id=1, source_target_pairs={{0,2},{2,4},{4,6},{6,8},{8,10},{10,12},{12,14},{14,0},{1,3},{3,5},... | collective-permute-start | bytes 1179656 | tf_op jit(solution)/shard_map/ppermute | solution.py:23
  39.5 59.8 %collective-permute-start.1 = (bf16[128,1536]{1,0:T(8,128)(2,1)}, bf16[128,1536]{1,0:T(8,128)(2,1)}, u32[]{:S(2)}, u32[]{:S(2)}) collective-permute-start(bf16[128,1536]{1,0:T(8,128)(2,1)} %pad_maximum_fusion), channel_id=1, source_target_pairs={{0,4},{2,6},{4,8},{6,10},{8,12},{10,14},{12,0},{14,2},{1,5},{3,7},... | collective-permute-start | bytes 1179656 | tf_op jit(solution)/shard_map/ppermute | solution.py:23
  43.5 140.7 %collective-permute-start.19 = (bf16[128,1536]{1,0:T(8,128)(2,1)}, bf16[128,1536]{1,0:T(8,128)(2,1)}, u32[]{:S(2)}, u32[]{:S(2)}) collective-permute-start(bf16[128,1536]{1,0:T(8,128)(2,1)} %pad_maximum_fusion.1), channel_id=1, source_target_pairs={{0,14},{2,0},{4,2},{6,4},{8,6},{10,8},{12,10},{14,12},{1,15},{3,1}... | collective-permute-start | bytes 1179656 | tf_op jit(solution)/shard_map/ppermute | solution.py:23
  83.0 116.3 %collective-permute-start.17 = (bf16[128,1536]{1,0:T(8,128)(2,1)}, bf16[128,1536]{1,0:T(8,128)(2,1)}, u32[]{:S(2)}, u32[]{:S(2)}) collective-permute-start(bf16[128,1536]{1,0:T(8,128)(2,1)} %pad_maximum_fusion.1), channel_id=1, source_target_pairs={{0,12},{2,14},{4,0},{6,2},{8,4},{10,6},{12,8},{14,10},{1,13},{3,15... | collective-permute-start | bytes 1179656 | tf_op jit(solution)/shard_map/ppermute | solution.py:23
  85.6 120.7 %collective-permute-start.15 = (bf16[128,1536]{1,0:T(8,128)(2,1)}, bf16[128,1536]{1,0:T(8,128)(2,1)}, u32[]{:S(2)}, u32[]{:S(2)}) collective-permute-start(bf16[128,1536]{1,0:T(8,128)(2,1)} %pad_maximum_fusion.1), channel_id=1, source_target_pairs={{0,10},{2,12},{4,14},{6,0},{8,2},{10,4},{12,6},{14,8},{1,11},{3,13... | collective-permute-start | bytes 1179656 | tf_op jit(solution)/shard_map/ppermute | solution.py:23
  97.4 116.4 %collective-permute-start.13 = (bf16[128,1536]{1,0:T(8,128)(2,1)}, bf16[128,1536]{1,0:T(8,128)(2,1)}, u32[]{:S(2)}, u32[]{:S(2)}) collective-permute-start(bf16[128,1536]{1,0:T(8,128)(2,1)} %pad_maximum_fusion.1), channel_id=1, source_target_pairs={{0,8},{2,10},{4,12},{6,14},{8,0},{10,2},{12,4},{14,6},{1,9},{3,11}... | collective-permute-start | bytes 1179656 | tf_op jit(solution)/shard_map/ppermute | solution.py:23
  99.2 21.4 %copy-start.17 = (bf16[128,768]{0,1:T(8,128)(2,1)}, bf16[128,768]{0,1:T(8,128)(2,1)S(1)}, u32[]{:S(2)}) copy-start(bf16[128,768]{0,1:T(8,128)(2,1)S(1)} %copy.125) | copy-start | bytes 589828
  99.3 118.1 %collective-permute-start.11 = (bf16[128,1536]{1,0:T(8,128)(2,1)}, bf16[128,1536]{1,0:T(8,128)(2,1)}, u32[]{:S(2)}, u32[]{:S(2)}) collective-permute-start(bf16[128,1536]{1,0:T(8,128)(2,1)} %pad_maximum_fusion.1), channel_id=1, source_target_pairs={{0,6},{2,8},{4,10},{6,12},{8,14},{10,0},{12,2},{14,4},{1,7},{3,9},... | collective-permute-start | bytes 1179656 | tf_op jit(solution)/shard_map/ppermute | solution.py:23
  177.3 156.3 %reduce-scatter.5.cloned.1.call-start = ((), (), s32[]{:S(2)}) async-start(), calls=%async_computation.3 | async-start | bytes 884736 | tf_op jit(solution)/shard_map/reduce_scatter | solution.py:106
  184.2 19.6 %copy-start.21 = (bf16[128,768]{0,1:T(8,128)(2,1)S(1)}, bf16[128,768]{0,1:T(8,128)(2,1)}, u32[]{:S(2)}) copy-start(bf16[128,768]{0,1:T(8,128)(2,1)} %copy.131) | copy-start | bytes 589828
  184.2 37.7 %collective-permute-start.7 = (bf16[128,1536]{1,0:T(8,128)(2,1)}, bf16[128,1536]{1,0:T(8,128)(2,1)}, u32[]{:S(2)}, u32[]{:S(2)}) collective-permute-start(bf16[128,1536]{1,0:T(8,128)(2,1)} %pad_maximum_fusion.1), channel_id=1, source_target_pairs={{0,2},{2,4},{4,6},{6,8},{8,10},{10,12},{12,14},{14,0},{1,3},{3,5},... | collective-permute-start | bytes 1179656 | tf_op jit(solution)/shard_map/ppermute | solution.py:23
  199.3 31.7 %collective-permute-start.9 = (bf16[128,1536]{1,0:T(8,128)(2,1)}, bf16[128,1536]{1,0:T(8,128)(2,1)}, u32[]{:S(2)}, u32[]{:S(2)}) collective-permute-start(bf16[128,1536]{1,0:T(8,128)(2,1)} %pad_maximum_fusion.1), channel_id=1, source_target_pairs={{0,4},{2,6},{4,8},{6,10},{8,12},{10,14},{12,0},{14,2},{1,5},{3,7},... | collective-permute-start | bytes 1179656 | tf_op jit(solution)/shard_map/ppermute | solution.py:23
  206.3 47.1 %collective-permute-start.20 = (f32[16,128]{1,0:T(8,128)}, f32[16,128]{1,0:T(8,128)}, u32[]{:S(2)}, u32[]{:S(2)}) collective-permute-start(f32[16,128]{1,0:T(8,128)} %pad_maximum_fusion.9), channel_id=1, source_target_pairs={{0,14},{2,0},{4,2},{6,4},{8,6},{10,8},{12,10},{14,12},{1,15},{3,1}... | collective-permute-start | bytes 24584 | tf_op jit(solution)/shard_map/ppermute | solution.py:23
  213.8 47.2 %collective-permute-start.18 = (f32[16,128]{1,0:T(8,128)}, f32[16,128]{1,0:T(8,128)}, u32[]{:S(2)}, u32[]{:S(2)}) collective-permute-start(f32[16,128]{1,0:T(8,128)} %pad_maximum_fusion.9), channel_id=1, source_target_pairs={{0,12},{2,14},{4,0},{6,2},{8,4},{10,6},{12,8},{14,10},{1,13},{3,15... | collective-permute-start | bytes 24584 | tf_op jit(solution)/shard_map/ppermute | solution.py:23
  217.4 50.4 %collective-permute-start.16 = (f32[16,128]{1,0:T(8,128)}, f32[16,128]{1,0:T(8,128)}, u32[]{:S(2)}, u32[]{:S(2)}) collective-permute-start(f32[16,128]{1,0:T(8,128)} %pad_maximum_fusion.9), channel_id=1, source_target_pairs={{0,10},{2,12},{4,14},{6,0},{8,2},{10,4},{12,6},{14,8},{1,11},{3,13... | collective-permute-start | bytes 24584 | tf_op jit(solution)/shard_map/ppermute | solution.py:23
  221.8 52.0 %collective-permute-start.14 = (f32[16,128]{1,0:T(8,128)}, f32[16,128]{1,0:T(8,128)}, u32[]{:S(2)}, u32[]{:S(2)}) collective-permute-start(f32[16,128]{1,0:T(8,128)} %pad_maximum_fusion.9), channel_id=1, source_target_pairs={{0,8},{2,10},{4,12},{6,14},{8,0},{10,2},{12,4},{14,6},{1,9},{3,11}... | collective-permute-start | bytes 24584 | tf_op jit(solution)/shard_map/ppermute | solution.py:23
  231.0 46.4 %collective-permute-start.12 = (f32[16,128]{1,0:T(8,128)}, f32[16,128]{1,0:T(8,128)S(1)}, u32[]{:S(2)}, u32[]{:S(2)}) collective-permute-start(f32[16,128]{1,0:T(8,128)} %pad_maximum_fusion.9), channel_id=1, source_target_pairs={{0,6},{2,8},{4,10},{6,12},{8,14},{10,0},{12,2},{14,4},{1,7},{3,9},... | collective-permute-start | bytes 24584 | tf_op jit(solution)/shard_map/ppermute | solution.py:23
  253.4 26.1 %collective-permute-start.8 = (f32[16,128]{1,0:T(8,128)}, f32[16,128]{1,0:T(8,128)S(1)}, u32[]{:S(2)}, u32[]{:S(2)}) collective-permute-start(f32[16,128]{1,0:T(8,128)} %pad_maximum_fusion.9), channel_id=1, source_target_pairs={{0,2},{2,4},{4,6},{6,8},{8,10},{10,12},{12,14},{14,0},{1,3},{3,5},... | collective-permute-start | bytes 24584 | tf_op jit(solution)/shard_map/ppermute | solution.py:23
  261.0 21.4 %collective-permute-start.10 = (f32[16,128]{1,0:T(8,128)}, f32[16,128]{1,0:T(8,128)S(1)}, u32[]{:S(2)}, u32[]{:S(2)}) collective-permute-start(f32[16,128]{1,0:T(8,128)} %pad_maximum_fusion.9), channel_id=1, source_target_pairs={{0,4},{2,6},{4,8},{6,10},{8,12},{10,14},{12,0},{14,2},{1,5},{3,7},... | collective-permute-start | bytes 24584 | tf_op jit(solution)/shard_map/ppermute | solution.py:23
  267.8 35.5 %collective-permute-start.27 = (bf16[128,960]{0,1:T(8,128)(2,1)}, bf16[128,960]{0,1:T(8,128)(2,1)}, u32[]{:S(2)}, u32[]{:S(2)}) collective-permute-start(bf16[128,960]{0,1:T(8,128)(2,1)} %get-tuple-element.81), channel_id=1, source_target_pairs={{0,14},{2,0},{4,2},{6,4},{8,6},{10,8},{12,10},{14,12},{1,15},{3,1}... | collective-permute-start | bytes 737288 | tf_op jit(solution)/shard_map/ppermute | solution.py:99
  273.8 30.7 %collective-permute-start.26 = (bf16[128,960]{0,1:T(8,128)(2,1)}, bf16[128,960]{0,1:T(8,128)(2,1)}, u32[]{:S(2)}, u32[]{:S(2)}) collective-permute-start(bf16[128,960]{0,1:T(8,128)(2,1)} %get-tuple-element.80), channel_id=1, source_target_pairs={{0,12},{2,14},{4,0},{6,2},{8,4},{10,6},{12,8},{14,10},{1,13},{3,15... | collective-permute-start | bytes 737288 | tf_op jit(solution)/shard_map/ppermute | solution.py:99
  277.3 28.4 %collective-permute-start.25 = (bf16[128,960]{0,1:T(8,128)(2,1)}, bf16[128,960]{0,1:T(8,128)(2,1)}, u32[]{:S(2)}, u32[]{:S(2)}) collective-permute-start(bf16[128,960]{0,1:T(8,128)(2,1)} %get-tuple-element.79), channel_id=1, source_target_pairs={{0,10},{2,12},{4,14},{6,0},{8,2},{10,4},{12,6},{14,8},{1,11},{3,13... | collective-permute-start | bytes 737288 | tf_op jit(solution)/shard_map/ppermute | solution.py:99
  279.5 33.6 %collective-permute-start.24 = (bf16[128,960]{0,1:T(8,128)(2,1)}, bf16[128,960]{0,1:T(8,128)(2,1)}, u32[]{:S(2)}, u32[]{:S(2)}) collective-permute-start(bf16[128,960]{0,1:T(8,128)(2,1)} %get-tuple-element.78), channel_id=1, source_target_pairs={{0,8},{2,10},{4,12},{6,14},{8,0},{10,2},{12,4},{14,6},{1,9},{3,11}... | collective-permute-start | bytes 737288 | tf_op jit(solution)/shard_map/ppermute | solution.py:99
  282.4 16.4 %collective-permute-start.21 = (bf16[128,960]{0,1:T(8,128)(2,1)}, bf16[128,960]{0,1:T(8,128)(2,1)}, u32[]{:S(2)}, u32[]{:S(2)}) collective-permute-start(bf16[128,960]{0,1:T(8,128)(2,1)} %get-tuple-element.82), channel_id=1, source_target_pairs={{0,2},{2,4},{4,6},{6,8},{8,10},{10,12},{12,14},{14,0},{1,3},{3,5},... | collective-permute-start | bytes 737288 | tf_op jit(solution)/shard_map/ppermute | solution.py:99
  298.8 18.6 %collective-permute-start.23 = (bf16[128,960]{0,1:T(8,128)(2,1)}, bf16[128,960]{0,1:T(8,128)(2,1)S(1)}, u32[]{:S(2)}, u32[]{:S(2)}) collective-permute-start(bf16[128,960]{0,1:T(8,128)(2,1)} %get-tuple-element.77), channel_id=1, source_target_pairs={{0,6},{2,8},{4,10},{6,12},{8,14},{10,0},{12,2},{14,4},{1,7},{3,9},... | collective-permute-start | bytes 737288 | tf_op jit(solution)/shard_map/ppermute | solution.py:99
  303.3 14.3 %collective-permute-start.22 = (bf16[128,960]{0,1:T(8,128)(2,1)S(1)}, bf16[128,960]{0,1:T(8,128)(2,1)S(1)}, u32[]{:S(2)}, u32[]{:S(2)}) collective-permute-start(bf16[128,960]{0,1:T(8,128)(2,1)S(1)} %copy-done.40), channel_id=1, source_target_pairs={{0,4},{2,6},{4,8},{6,10},{8,12},{10,14},{12,0},{14,2},{1,5},{3,7},... | collective-permute-start | bytes 737288 | tf_op jit(solution)/shard_map/ppermute | solution.py:99
  (55 other events, 438.2 us)
Sparse Core Ops, SparseCore 0:
  177.4 15.2 reduce-scatter.2
  319.0 14.6 reduce-scatter.4

commit v3 on v1

--- a/solution.py
+++ b/solution.py
@@ -86,12 +86,18 @@
         partial_out.astype(jnp.bfloat16), "tensor", scatter_dimension=1, tiled=True
     ).astype(jnp.float32)
     block_out = (residual[0].astype(jnp.float32) + mixed).astype(jnp.bfloat16)
+    n_seq = lax.axis_size("seq")
+    n_dp = lax.axis_size("dp")
+    col_width = grad_full.shape[1] // (n_dp * n_seq)
+    g_cols = jnp.transpose(grad_full.reshape(frames_here, n_dp, n_seq, col_width), (0, 2, 1, 3))
+    g_mine = lax.all_to_all(
+        g_cols.reshape(frames_here, n_seq * n_dp * col_width), "seq", 1, 0, tiled=True
+    )
+    attn_all = lax.all_gather(attn, "seq", axis=0, tiled=True)
     weight_term = lax.dot_general(
-        attn, grad_full, (((0,), (0,)), ((), ())), preferred_element_type=jnp.float32
+        attn_all, g_mine, (((0,), (0,)), ((), ())), preferred_element_type=jnp.float32
     )
-    grad_weight = lax.psum_scatter(
-        weight_term.astype(jnp.bfloat16), ("dp", "seq"), scatter_dimension=1, tiled=True
-    ).astype(jnp.float32)
+    grad_weight = lax.psum_scatter(weight_term, "dp", scatter_dimension=1, tiled=True)
     g_heads = split_heads(grad_attn)
     delta = jnp.sum(jnp.transpose(g_heads, (1, 0, 2)).astype(jnp.float32) * attn_full, axis=2)
 
@@ -110,7 +116,15 @@
 
     empty_q = jnp.zeros((heads_here, frames_here, HEAD_DIM), jnp.float32)
     grad_q = by_blocks(query_step, empty_q, (k_all, v_all))
-    stats = lax.all_gather(jnp.concatenate([log_sum, delta], axis=0), "seq", axis=1, tiled=True)
+    stats = lax.psum(
+        lax.dynamic_update_slice_in_dim(
+            jnp.zeros((2 * heads_here, n_seq * frames_here), jnp.float32),
+            jnp.concatenate([log_sum, delta], axis=0),
+            lax.axis_index("seq") * frames_here,
+            axis=1,
+        ),
+        "seq",
+    )
 
     def key_step(state, part, start):
         grad_k, grad_v = state

time: 286 us -> 289 us (1.010)
  blocking collectives: 33.1 us -> 2.21 us
  waiting for transfers between devices: 178 us -> 206 us
  local copies, waits for them, and re-layouts: 21.1 us -> 25.1 us
  starting transfers between devices: 0.16 us -> 3.88 us
    reduce_scatter x1, waiting for transfers between devices: 86.8 us -> 11.3 us  [shards(): lax.psum_scatter(weight_term, 'dp', scatter_dimension=1, tiled=True)]
    psum x0 -> x1, waiting for transfers between devices: none -> 50.8 us  [shards(): lax.psum(lax.dynamic_update_slice_in_dim(jnp.zeros((2 * heads_here, n_seq...]
    all_gather x0 -> x1, waiting for transfers between devices: none -> 46.1 us  [shards(): attn_all = lax.all_gather(attn, 'seq', axis=0, tiled=True)]
    all_gather x1 -> x0, blocking collectives: 30.7 us -> none  [shards(): lax.all_gather(jnp.concatenate([log_sum, delta], axis=0), 'seq', axis=1,...]
    all_gather x1, waiting for transfers between devices: 32.7 us -> 39.3 us  [shards(): lax.all_gather(jnp.concatenate([own_q, grad_attn], axis=1), 'seq', axis=0...]
    all_to_all x0 -> x1, starting transfers between devices: none -> 3.45 us  [shards(): lax.all_to_all(g_cols.reshape(frames_here, n_seq * n_dp * col_width), 'se...]
  transfers between devices with their start and end apart: 4 -> 7, of which waited for: 3 -> 5; matrix products, arithmetic and copies ran while one was open for 20% -> 20% of each run, Pallas kernels for 0% -> 0%
where the time goes in v3:
time: 289 us; the launch traced here: 288 us
  waiting for transfers between devices  206 us (71%)
  matrix products  31 us (11%)
  local copies, waits for them, and re-layouts  25.1 us (9%)
  between operations  15 us (5%)
  other arithmetic  5.46 us (2%)
  starting transfers between devices  3.88 us (1%)
    all_gather x1, waiting for transfers between devices, shards(): lax.all_gather(jnp.concatenate([own_k, own_v], axis=1), 'seq', axis=0, ti...  57.6 us
    psum x1, waiting for transfers between devices, shards(): lax.psum(lax.dynamic_update_slice_in_dim(jnp.zeros((2 * heads_here, n_seq...  50.8 us
    all_gather x1, waiting for transfers between devices, shards(): attn_all = lax.all_gather(attn, 'seq', axis=0, tiled=True)  46.1 us
    all_gather x1, waiting for transfers between devices, shards(): lax.all_gather(jnp.concatenate([own_q, grad_attn], axis=1), 'seq', axis=0...  39.3 us
    reduce_scatter x1, waiting for transfers between devices, shards(): lax.psum_scatter(weight_term, 'dp', scatter_dimension=1, tiled=True)  11.3 us
    dot_general x2, matrix products, masked_scores(): jnp.einsum('ihc,jhc->hij', left, right, preferred_element_type=jnp.float32)  7.09 us
    slice x2, local copies, waits for them, and re-layouts, shards(): k_all = kv_all[:, :width]  6.42 us
    slice x2, local copies, waits for them, and re-layouts, shards(): qg_all[:, width:]  6.35 us
  transfers between devices with their start and end apart: 7, of which 5 were waited for; matrix products, arithmetic and copies ran while one was open for 20% of the time, Pallas kernels for 0%

profile of v3, /device:TPU:0, one launch (start us, length us, event | category | flops | bytes accessed | tf_op | source)
XLA Modules:
  0.0 288.2 jit_solution(5828975553397593760)
XLA Ops:
  7.2 2.0 pad_maximum_fusion
  9.3 1.1 copy.29
  10.4 2.2 all-gather
  12.6 0.9 convolution_convert_fusion.1
  13.5 0.8 pad_maximum_fusion.1
  15.4 57.6 %all-gather.5.cloned.1.call-done = bf16[1024,1536]{1,0:T(8,128)(2,1)} async-done(((bf16[128,1536]{1,0:T(8,128)(2,1)}), bf16[1024,1536]{1,0:T(8,128)(2,1)}) %all-gather.5.cloned.1.call-update) | async-done | bytes 3145744 | tf_op jit(solution)/shard_map/all_gather | solution.py:76
  73.0 3.8 %fusion.46 = (bf16[1024,768]{1,0:T(8,128)(2,1)}, bf16[1024,768]{1,0:T(8,128)(2,1)}) fusion(bf16[1024,1536]{1,0:T(8,128)(2,1)} %all-gather.5.cloned.1.call-done), kind=kLoop, calls=%fused_computation.62 | loop fusion | bytes 6291456 | tf_op jit(solution)/shard_map/slice | solution.py:78
  76.8 2.6 copy.25
  79.4 2.6 copy.27
  82.0 2.9 bitcast_reduce_fusion
  84.9 0.9 fusion.5
  85.8 3.5 %fusion.33 = (bf16[128,8,96]{0,2,1:T(8,128)(2,1)}, f32[8,128,96]{1,2,0:T(8,128)S(1)}) fusion(f32[128,8]{0,1:T(8,128)S(1)} %bitcast_add_fusion.1, f32[128,8]{0,1:T(8,128)S(1)} %get-tuple-element.104, bf16[1024,8,96]{0,2,1:T(8,128)(2,1)S(1)} %bitcast.104, f32[8,1024,128]{2,1,0:T(8,128)S(1)} %get-tuple-element.107, f32[8,128]{1,0:T(8,128)S(1)} %broadcast_maximum_fusion, ...), kind=kOutput, calls=%fused_computation.42 | convolution fusion | flops 1211400192 | bytes 6370304 | tf_op jit(solution)/shard_map/while/body/eval_jaxpr/hij,jhc->hic/dot_general | solution.py:61
  90.7 0.8 copy.36
  91.5 3.5 %all-to-all-start = ((bf16[128,8,192]{0,2,1:T(8,128)(2,1)}), bf16[128,8,192]{0,2,1:T(8,128)(2,1)S(1)}, u32[]{:S(2)}, u32[]{:S(2)}) async-start(bf16[128,8,192]{0,2,1:T(8,128)(2,1)} %bitcast.29), calls=%async_computation.1 | async-start | bytes 786432 | tf_op jit(solution)/shard_map/all_to_all | solution.py:93
  95.2 0.8 copy.35
  96.0 39.3 %all-gather.7.cloned.1.call-done = bf16[1024,1536]{1,0:T(8,128)(2,1)} async-done(((bf16[128,1536]{1,0:T(8,128)(2,1)}), bf16[1024,1536]{1,0:T(8,128)(2,1)}) %all-gather.7.cloned.1.call-update) | async-done | bytes 3145744 | tf_op jit(solution)/shard_map/all_gather | solution.py:77
  135.3 3.8 %fusion.45 = (bf16[1024,768]{1,0:T(8,128)(2,1)}, bf16[1024,768]{1,0:T(8,128)(2,1)}) fusion(bf16[1024,1536]{1,0:T(8,128)(2,1)} %all-gather.7.cloned.1.call-done), kind=kLoop, calls=%fused_computation.61 | loop fusion | bytes 6291456 | tf_op jit(solution)/shard_map/slice | solution.py:151
  139.0 5.6 %fusion.21 = bf16[8,128,96]{1,2,0:T(8,128)(2,1)S(1)} fusion(bf16[1024,8,96]{0,2,1:T(8,128)(2,1)} %bitcast.99, f32[8,1024,128]{2,1,0:T(8,128)} %copy-done.1, bf16[128,8,96]{0,2,1:T(8,128)(2,1)S(1)} %bitcast.115, bf16[1024,8,96]{0,2,1:T(8,128)(2,1)} %bitcast.103, f32[8,128]{1,0:T(8,128)S(1)} %fusion.30, f32[8,128]{1,0:T(8,128)S(1)} %get-tuple-element.102, ...), kind=kOutput, calls=%fused_computation.26 | convolution fusion | flops 410091520 | bytes 7742464 | tf_op jit(solution)/shard_map/while/body/eval_jaxpr/hij,jhc->hic/dot_general | solution.py:113
  144.7 1.3 convolution_convert_fusion
  145.9 0.8 copy.38
  146.8 2.6 copy.32
  149.4 2.6 copy.34
  152.2 4.2 %fusion.48 = f32[8,1024,128]{2,1,0:T(8,128)} fusion(bf16[1024,8,96]{0,2,1:T(8,128)(2,1)} %bitcast.100, bf16[128,8,96]{0,2,1:T(8,128)(2,1)S(1)} %bitcast.108), kind=kOutput, calls=%fused_computation.64 | convolution fusion | flops 201326592 | bytes 5963776 | tf_op jit(solution)/shard_map/while/body/eval_jaxpr/ihc,jhc->hij/dot_general | solution.py:49
  156.5 50.8 %all-reduce.2.cloned.1.call-done = f32[16,1024]{1,0:T(8,128)} async-done(((f32[16,1024]{1,0:T(8,128)}), f32[16,1024]{1,0:T(8,128)}) %all-reduce.2.cloned.1.call-update) | async-done | bytes 65552 | tf_op jit(solution)/shard_map/psum | solution.py:119
  208.0 46.1 %all-gather.9.cloned.1.call-done = bf16[1024,768]{0,1:T(8,128)(2,1)} async-done(((bf16[128,768]{0,1:T(8,128)(2,1)}), bf16[1024,768]{0,1:T(8,128)(2,1)}) %all-gather.9.cloned.1.call-update) | async-done | bytes 1572880 | tf_op jit(solution)/shard_map/all_gather | solution.py:96
  254.1 2.9 %fusion.26 = f32[768,192]{0,1:T(8,128)} fusion(bf16[1024,768]{0,1:T(8,128)(2,1)} %all-gather.9.cloned.1.call-done, bf16[128,8,192]{0,2,1:T(8,128)(2,1)S(1)} %all-to-all-done), kind=kOutput, calls=%fused_computation.30 | convolution fusion | flops 301989888 | bytes 2555904 | tf_op jit(solution)/shard_map/dot_general | solution.py:97
  257.0 6.2 %fusion.22 = bf16[8,128,96]{1,2,0:T(8,128)(2,1)S(1)} fusion(bf16[1024,8,96]{0,2,1:T(8,128)(2,1)} %bitcast.101, f32[8,1024,128]{2,1,0:T(8,128)} %fusion.48, bf16[1024,8,96]{0,2,1:T(8,128)(2,1)} %bitcast.105, bf16[128,8,96]{0,2,1:T(8,128)(2,1)S(1)} %bitcast.116, f32[8,1024]{1,0:T(8,128)S(1)} %get-tuple-element.101, f32[8,1024]{1,0:T(8,128)S(1)} %get-tuple-element.100, ...), kind=kOutput, calls=%fused_computation.27 | convolution fusion | flops 410091520 | bytes 7798912 | tf_op jit(solution)/shard_map/while/body/eval_jaxpr/hij,ihc->hjc/dot_general | solution.py:138
  263.2 0.8 copy.39
  264.0 3.6 %fusion.23 = bf16[8,128,96]{1,2,0:T(8,128)(2,1)S(1)} fusion(bf16[1024,8,96]{0,2,1:T(8,128)(2,1)} %bitcast.106, f32[8,1024,128]{2,1,0:T(8,128)} %fusion.48, f32[8,1024]{1,0:T(8,128)S(1)} %get-tuple-element.100, pred[128]{0:T(512)(128)(4,1)S(1)} %add_compare_fusion), kind=kOutput, calls=%fused_computation.28 | convolution fusion | flops 205619200 | bytes 5996672 | tf_op jit(solution)/shard_map/while/body/eval_jaxpr/hij,ihc->hjc/dot_general | solution.py:141
  267.6 0.8 copy.40
  268.4 1.7 fusion.34
  270.1 11.3 %reduce-scatter.5.cloned.1.call-done = f32[768,96]{0,1:T(8,128)} async-done(((f32[768,192]{0,1:T(8,128)}), f32[768,96]{0,1:T(8,128)}) %reduce-scatter.5.cloned.1.call-update) | async-done | bytes 294928 | tf_op jit(solution)/shard_map/reduce_scatter | solution.py:100
  (46 shorter events, 3.1 us)
Async XLA Ops:
  7.2 5.4 %copy-start = (bf16[768,1536]{1,0:T(8,128)(2,1)S(1)}, bf16[768,1536]{1,0:T(8,128)(2,1)}, u32[]{:S(2)}) copy-start(bf16[768,1536]{1,0:T(8,128)(2,1)} %param.10) | copy-start | bytes 7077892
  7.2 6.3 %copy-start.4 = (bf16[1,128,768]{2,1,0:T(8,128)(2,1)S(1)}, bf16[1,128,768]{2,1,0:T(8,128)(2,1)}, u32[]{:S(2)}) copy-start(bf16[1,128,768]{2,1,0:T(8,128)(2,1)} %param.7) | copy-start | bytes 589828
  7.2 65.8 %all-gather.5.cloned.1.call-start = ((), (), s32[]{:S(2)}) async-start(), calls=%async_computation.3 | async-start | bytes 3538944 | tf_op jit(solution)/shard_map/all_gather | solution.py:76
  9.2 126.0 %all-gather.7.cloned.1.call-start = ((), (), s32[]{:S(2)}) async-start(), calls=%async_computation.5 | async-start | bytes 3538944 | tf_op jit(solution)/shard_map/all_gather | solution.py:77
  14.3 192.9 %all-reduce.2.cloned.1.call-start = ((), (), s32[]{:S(2)}) async-start(), calls=%async_computation.6 | async-start | bytes 131072 | tf_op jit(solution)/shard_map/psum | solution.py:119
  82.0 3.9 %copy-start.2 = (bf16[1024,768]{0,1:T(8,128)(2,1)S(1)}, bf16[1024,768]{0,1:T(8,128)(2,1)}, u32[]{:S(2)}) copy-start(bf16[1024,768]{0,1:T(8,128)(2,1)} %copy.27) | copy-start | bytes 4718596
  84.8 4.5 %copy-start.1 = (f32[8,1024,128]{2,1,0:T(8,128)}, f32[8,1024,128]{2,1,0:T(8,128)S(1)}, u32[]{:S(2)}) copy-start(f32[8,1024,128]{2,1,0:T(8,128)S(1)} %get-tuple-element.107) | copy-start | bytes 12582916
  85.8 9.2 %copy-start.5 = (bf16[1,128,768]{2,1,0:T(8,128)(2,1)S(1)}, bf16[1,128,768]{2,1,0:T(8,128)(2,1)}, u32[]{:S(2)}) copy-start(bf16[1,128,768]{2,1,0:T(8,128)(2,1)} %param.8) | copy-start | bytes 589828
  85.8 9.4 %copy-start.6 = (bf16[1,128,768]{2,1,0:T(8,128)(2,1)S(1)}, bf16[1,128,768]{2,1,0:T(8,128)(2,1)}, u32[]{:S(2)}) copy-start(bf16[1,128,768]{2,1,0:T(8,128)(2,1)} %param.9) | copy-start | bytes 589828
  89.5 0.6 copy-start.7
  90.1 163.9 %all-gather.9.cloned.1.call-start = ((), (), s32[]{:S(2)}) async-start(), calls=%async_computation.7 | async-start | bytes 1769472 | tf_op jit(solution)/shard_map/all_gather | solution.py:96
  91.5 116.5 %all-to-all-start = ((bf16[128,8,192]{0,2,1:T(8,128)(2,1)}), bf16[128,8,192]{0,2,1:T(8,128)(2,1)S(1)}, u32[]{:S(2)}, u32[]{:S(2)}) async-start(bf16[128,8,192]{0,2,1:T(8,128)(2,1)} %bitcast.29), calls=%async_computation.1 | async-start | bytes 786432 | tf_op jit(solution)/shard_map/all_to_all | solution.py:93
  95.0 173.5 %reduce-scatter.3.cloned.1.call-start = ((), (), s32[]{:S(2)}) async-start(), calls=%async_computation.4 | async-start | bytes 589824 | tf_op jit(solution)/shard_map/reduce_scatter | solution.py:85
  139.0 5.6 %copy-start.3 = (bf16[128,8,96]{0,2,1:T(8,128)(2,1)S(1)}, bf16[128,8,96]{0,2,1:T(8,128)(2,1)}, u32[]{:S(2)}) copy-start(bf16[128,8,96]{0,2,1:T(8,128)(2,1)} %get-tuple-element.108) | copy-start | bytes 589828
  152.0 129.4 %reduce-scatter.5.cloned.1.call-start = ((), (), s32[]{:S(2)}) async-start(), calls=%async_computation.8 | async-start | bytes 884736 | tf_op jit(solution)/shard_map/reduce_scatter | solution.py:100
  152.2 104.8 %copy-start.8 = (bf16[1,128,768]{1,2,0:T(8,128)(2,1)S(1)}, bf16[1,128,768]{1,2,0:T(8,128)(2,1)}, u32[]{:S(2)}) copy-start(bf16[1,128,768]{1,2,0:T(8,128)(2,1)} %copy.35) | copy-start | bytes 589828
  263.2 5.2 %copy-start.9 = (bf16[1,128,768]{2,1,0:T(8,128)(2,1)S(1)}, bf16[1,128,768]{2,1,0:T(8,128)(2,1)}, u32[]{:S(2)}) copy-start(bf16[1,128,768]{2,1,0:T(8,128)(2,1)} %param.11) | copy-start | bytes 589828
Sparse Core Ops, SparseCore 0:
  10.2 62.7 all-gather.4
  75.1 60.0 all-gather.6
  139.3 67.9 all-reduce.1
  209.7 44.3 all-gather.8
  256.2 5.9 reduce-scatter.2
  264.9 16.4 reduce-scatter.4

commit v4 on v3

--- a/solution.py
+++ b/solution.py
@@ -17,6 +17,19 @@
 
 def join_heads(blocks):
     return jnp.transpose(blocks, (1, 0, 2)).reshape(blocks.shape[1], -1)
+
+
+def gather_rows(x, axis_name):
+    n = lax.axis_size(axis_name)
+    spread = jnp.broadcast_to(x[None], (n,) + x.shape)
+    return lax.all_to_all(spread, axis_name, 0, 0, tiled=True)
+
+
+def scatter_sum(x, axis_name, axis):
+    n = lax.axis_size(axis_name)
+    shape = x.shape[:axis] + (n, x.shape[axis] // n) + x.shape[axis + 1:]
+    pieces = jnp.moveaxis(x.reshape(shape), axis, 0)
+    return jnp.sum(lax.all_to_all(pieces, axis_name, 0, 0, tiled=True), axis=0)
 
 
 def by_blocks(step_fn, carry, piece):
@@ -73,8 +86,8 @@
         grad_full, out_weight, (((1,), (1,)), ((), ())), preferred_element_type=jnp.float32
     ).astype(jnp.bfloat16)
     width = own_k.shape[1]
-    kv_all = lax.all_gather(jnp.concatenate([own_k, own_v], axis=1), "seq", axis=0, tiled=True)
-    qg_all = lax.all_gather(jnp.concatenate([own_q, grad_attn], axis=1), "seq", axis=0, tiled=True)
+    kv_all = gather_rows(jnp.concatenate([own_k, own_v], axis=1), "seq").reshape(-1, 2 * own_k.shape[1])
+    qg_all = gather_rows(jnp.concatenate([own_q, grad_attn], axis=1), "seq").reshape(-1, 2 * own_k.shape[1])
     k_all = kv_all[:, :width]
     v_all = kv_all[:, width:]
     run_max, run_sum, total = by_blocks(forward_step, start_state, (k_all, v_all))
@@ -82,9 +95,7 @@
     attn_full = total / run_sum[:, :, None]
     attn = join_heads(attn_full).astype(jnp.bfloat16)
     partial_out = jnp.dot(attn, out_weight, preferred_element_type=jnp.float32)
-    mixed = lax.psum_scatter(
-        partial_out.astype(jnp.bfloat16), "tensor", scatter_dimension=1, tiled=True
-    ).astype(jnp.float32)
+    mixed = scatter_sum(partial_out, "tensor", 1)
     block_out = (residual[0].astype(jnp.float32) + mixed).astype(jnp.bfloat16)
     n_seq = lax.axis_size("seq")
     n_dp = lax.axis_size("dp")
@@ -93,11 +104,11 @@
     g_mine = lax.all_to_all(
         g_cols.reshape(frames_here, n_seq * n_dp * col_width), "seq", 1, 0, tiled=True
     )
-    attn_all = lax.all_gather(attn, "seq", axis=0, tiled=True)
+    attn_all = gather_rows(attn, "seq").reshape(-1, attn.shape[1])
     weight_term = lax.dot_general(
         attn_all, g_mine, (((0,), (0,)), ((), ())), preferred_element_type=jnp.float32
     )
-    grad_weight = lax.psum_scatter(weight_term, "dp", scatter_dimension=1, tiled=True)
+    grad_weight = scatter_sum(weight_term, "dp", 1)
     g_heads = split_heads(grad_attn)
     delta = jnp.sum(jnp.transpose(g_heads, (1, 0, 2)).astype(jnp.float32) * attn_full, axis=2)
 
@@ -116,15 +127,8 @@
 
     empty_q = jnp.zeros((heads_here, frames_here, HEAD_DIM), jnp.float32)
     grad_q = by_blocks(query_step, empty_q, (k_all, v_all))
-    stats = lax.psum(
-        lax.dynamic_update_slice_in_dim(
-            jnp.zeros((2 * heads_here, n_seq * frames_here), jnp.float32),
-            jnp.concatenate([log_sum, delta], axis=0),
-            lax.axis_index("seq") * frames_here,
-            axis=1,
-        ),
-        "seq",
-    )
+    stats = gather_rows(jnp.concatenate([log_sum, delta], axis=0), "seq")
+    stats = jnp.transpose(stats, (1, 0, 2)).reshape(2 * heads_here, -1)
 
     def key_step(state, part, start):
         grad_k, grad_v = state

time: 289 us -> 261 us (0.903)
  waiting for transfers between devices: 206 us -> 133 us
  starting transfers between devices: 3.88 us -> 29.2 us
  local copies, waits for them, and re-layouts: 25.1 us -> 47.5 us
  between operations: 15 us -> 1.6 us
  blocking collectives: 2.21 us -> 7.57 us
    all_gather x3 -> x0, waiting for transfers between devices: 143 us -> none  [the longest x1 57.6 us: shards(): lax.all_gather(jnp.concatenate([own_k, own_v], axis=1), 'seq', axis=0, ti...]
    all_to_all x0 -> x5, waiting for transfers between devices: none -> 133 us  [the longest x4 130 us: gather_rows(): return lax.all_to_all(spread, axis_name, 0, 0, tiled=True)]
    psum x1 -> x0, waiting for transfers between devices: 50.8 us -> none  [shards(): lax.psum(lax.dynamic_update_slice_in_dim(jnp.zeros((2 * heads_here, n_seq...]
    all_to_all x0 -> x5, starting transfers between devices: none -> 25.5 us  [the longest x4 22 us: gather_rows(): return lax.all_to_all(spread, axis_name, 0, 0, tiled=True)]
    reduce_scatter x2 -> x0, waiting for transfers between devices: 11.3 us -> none  [the longest x1 11.3 us: shards(): lax.psum_scatter(weight_term, 'dp', scatter_dimension=1, tiled=True)]
    broadcast_in_dim x1 -> x4, local copies, waits for them, and re-layouts: 0.01 us -> 6.95 us  [gather_rows(): spread = jnp.broadcast_to(x[None], (n,) + x.shape)]
    all_to_all x0 -> x3, local copies, waits for them, and re-layouts: none -> 6.47 us  [the longest x2 5.67 us: gather_rows(): return lax.all_to_all(spread, axis_name, 0, 0, tiled=True)]
    unnamed x27 -> x51, local copies, waits for them, and re-layouts: 5.38 us -> 11.2 us
  transfers between devices with their start and end apart: 7 -> 6, of which waited for: 5 -> 5; matrix products, arithmetic and copies ran while one was open for 20% -> 28% of each run, Pallas kernels for 0% -> 0%
where the time goes in v4:
time: 261 us; the launch traced here: 260 us
  waiting for transfers between devices  133 us (51%)
  local copies, waits for them, and re-layouts  47.5 us (18%)
  matrix products  32.7 us (13%)
  starting transfers between devices  29.2 us (11%)
  other arithmetic  7.89 us (3%)
  blocking collectives  7.57 us (3%)
    all_to_all x4, waiting for transfers between devices, gather_rows(): return lax.all_to_all(spread, axis_name, 0, 0, tiled=True)  130 us
    all_to_all x4, starting transfers between devices, gather_rows(): return lax.all_to_all(spread, axis_name, 0, 0, tiled=True)  22 us
    unnamed x51, local copies, waits for them, and re-layouts  11.2 us
    broadcast_in_dim x4, local copies, waits for them, and re-layouts, gather_rows(): spread = jnp.broadcast_to(x[None], (n,) + x.shape)  6.95 us
    dot_general x1, matrix products, forward_step(): jnp.einsum('hij,jhc->hic', weights, split_heads(v_rows).astype(jnp.float3...  6.39 us
    dot_general x1, matrix products, key_step(): jnp.einsum('hij,ihc->hjc', dscores, q_part, preferred_element_type=jnp.fl...  5.96 us
    dot_general x1, matrix products, query_step(): jnp.einsum('hij,jhc->hic', dscores, split_heads(k_rows), preferred_elemen...  5.7 us
    all_to_all x2, local copies, waits for them, and re-layouts, gather_rows(): return lax.all_to_all(spread, axis_name, 0, 0, tiled=True)  5.67 us
  transfers between devices with their start and end apart: 6, of which 5 were waited for; matrix products, arithmetic and copies ran while one was open for 28% of the time, Pallas kernels for 0%

profile of v4, /device:TPU:0, one launch (start us, length us, event | category | flops | bytes accessed | tf_op | source)
XLA Modules:
  0.0 259.7 jit_solution(360311528594868547)
XLA Ops:
  1.9 2.0 broadcast_in_dim.91
  4.0 7.4 %all-to-all-start = ((bf16[8,128,1536]{1,2,0:T(8,128)(2,1)}), bf16[8,128,1536]{1,2,0:T(8,128)(2,1)S(1)}, u32[]{:S(2)}, u32[]{:S(2)}) async-start(bf16[8,128,1536]{1,2,0:T(8,128)(2,1)} %broadcast_in_dim.91), calls=%async_computation | async-start | bytes 6291456 | tf_op jit(solution)/shard_map/all_to_all | solution.py:25
  12.9 4.3 %copy.106 = bf16[1536,768]{1,0:T(8,128)(2,1)} copy(bf16[1536,768]{0,1:T(8,128)(2,1)} %bitcast.119) | data formatting | bytes 4718592 | tf_op jit(solution)/shard_map/dot_general | solution.py:97
  18.0 2.4 all-gather
  20.4 2.6 convolution_convert_fusion
  24.5 1.9 copy.89
  27.2 54.9 %all-to-all-done = bf16[8,128,1536]{1,2,0:T(8,128)(2,1)S(1)} async-done(((bf16[8,128,1536]{1,2,0:T(8,128)(2,1)}), bf16[8,128,1536]{1,2,0:T(8,128)(2,1)S(1)}, u32[]{:S(2)}, u32[]{:S(2)}) %all-to-all-start) | async-done | bytes 3145760 | tf_op jit(solution)/shard_map/all_to_all | solution.py:25
  82.1 3.6 %all-to-all-start.5 = ((bf16[128,8,192]{0,2,1:T(8,128)(2,1)}), bf16[128,8,192]{0,2,1:T(8,128)(2,1)S(1)}, u32[]{:S(2)}, u32[]{:S(2)}) async-start(bf16[128,8,192]{0,2,1:T(8,128)(2,1)} %bitcast.130), calls=%async_computation.5 | async-start | bytes 786432 | tf_op jit(solution)/shard_map/all_to_all | solution.py:104
  85.7 2.8 %copy.78 = bf16[8,128,1536]{2,1,0:T(8,128)(2,1)} copy(bf16[8,128,1536]{1,2,0:T(8,128)(2,1)S(1)} %all-to-all-done) | data formatting | bytes 6291456 | tf_op jit(solution)/shard_map/all_to_all | solution.py:25
  88.6 3.3 %fusion.42 = (bf16[1024,768]{1,0:T(8,128)(2,1)}, bf16[1024,768]{1,0:T(8,128)(2,1)S(1)}) fusion(bf16[1024,1536]{1,0:T(8,128)(2,1)} %bitcast.117), kind=kLoop, calls=%fused_computation.62 | loop fusion | bytes 6291456 | tf_op jit(solution)/shard_map/slice | solution.py:91
  93.6 2.4 bitcast_reduce_fusion
  96.0 1.9 copy-done
  100.3 6.4 %fusion.30 = (bf16[128,8,96]{0,2,1:T(8,128)(2,1)S(1)}, f32[8,128,96]{1,2,0:T(8,128)}) fusion(f32[128,8]{0,1:T(8,128)S(1)} %bitcast_add_fusion.2, f32[128,8]{0,1:T(8,128)} %get-tuple-element.131, bf16[1024,8,96]{0,2,1:T(8,128)(2,1)S(1)} %bitcast.126, f32[8,1024,128]{2,1,0:T(8,128)} %copy-done, f32[8,128]{1,0:T(8,128)S(1)} %broadcast_maximum_fusion, ...), kind=kOutput, calls=%fused_computation.41 | convolution fusion | flops 1211400192 | bytes 6370304 | tf_op jit(solution)/shard_map/while/body/eval_jaxpr/hij,jhc->hic/dot_general | solution.py:74
  107.6 5.1 %all_to_all.49 = f32[2,128,768]{2,1,0:T(8,128)} all-to-all(f32[2,128,768]{2,1,0:T(8,128)S(1)} %convolution_bitcast_fusion), channel_id=1, replica_groups=mesh['dp'=2,'seq'=8,'tensor'=2] {'tensor'}, dimensions={0} | all-to-all | bytes 1572864 | tf_op jit(solution)/shard_map/all_to_all | solution.py:32
  112.8 2.1 broadcast_in_dim.94
  114.9 6.1 %all-to-all-start.2 = ((bf16[8,128,1536]{1,2,0:T(8,128)(2,1)}), bf16[8,128,1536]{1,2,0:T(8,128)(2,1)S(1)}, u32[]{:S(2)}, u32[]{:S(2)}) async-start(bf16[8,128,1536]{1,2,0:T(8,128)(2,1)} %broadcast_in_dim.94), calls=%async_computation.2 | async-start | bytes 6291456 | tf_op jit(solution)/shard_map/all_to_all | solution.py:25
  123.0 69.0 %all-to-all-done.2 = bf16[8,128,1536]{1,2,0:T(8,128)(2,1)S(1)} async-done(((bf16[8,128,1536]{1,2,0:T(8,128)(2,1)}), bf16[8,128,1536]{1,2,0:T(8,128)(2,1)S(1)}, u32[]{:S(2)}, u32[]{:S(2)}) %all-to-all-start.2) | async-done | bytes 3145760 | tf_op jit(solution)/shard_map/all_to_all | solution.py:25
  192.6 4.0 %all-to-all-start.3 = ((f32[8,16,128]{2,1,0:T(8,128)}), f32[8,16,128]{2,1,0:T(8,128)}, u32[]{:S(2)}, u32[]{:S(2)}) async-start(f32[8,16,128]{2,1,0:T(8,128)} %broadcast_in_dim.95), calls=%async_computation.3 | async-start | bytes 131072 | tf_op jit(solution)/shard_map/all_to_all | solution.py:25
  198.4 5.2 %all-to-all-done.3 = f32[8,16,128]{2,1,0:T(8,128)} async-done(((f32[8,16,128]{2,1,0:T(8,128)}), f32[8,16,128]{2,1,0:T(8,128)}, u32[]{:S(2)}, u32[]{:S(2)}) %all-to-all-start.3) | async-done | bytes 65568 | tf_op jit(solution)/shard_map/all_to_all | solution.py:25
  203.5 2.2 broadcast_in_dim.96
  205.7 4.5 %all-to-all-start.4 = ((bf16[8,128,768]{2,1,0:T(8,128)(2,1)}), bf16[8,128,768]{2,1,0:T(8,128)(2,1)}, u32[]{:S(2)}, u32[]{:S(2)}) async-start(bf16[8,128,768]{2,1,0:T(8,128)(2,1)} %broadcast_in_dim.96), calls=%async_computation.4 | async-start | bytes 3145728 | tf_op jit(solution)/shard_map/all_to_all | solution.py:25
  214.5 5.7 %fusion.21 = bf16[8,128,96]{1,2,0:T(8,128)(2,1)S(1)} fusion(bf16[1024,8,96]{0,2,1:T(8,128)(2,1)} %bitcast.122, f32[8,1024,128]{2,1,0:T(8,128)} %copy-done, bf16[128,8,96]{0,2,1:T(8,128)(2,1)} %bitcast.139, bf16[1024,8,96]{0,2,1:T(8,128)(2,1)} %bitcast.127, f32[8,128]{1,0:T(8,128)S(1)} %fusion.26, f32[8,128]{1,0:T(8,128)S(1)} %copy-done.19, ...), kind=kOutput, calls=%fused_computation.27 | convolution fusion | flops 410091520 | bytes 7742464 | tf_op jit(solution)/shard_map/while/body/eval_jaxpr/hij,jhc->hic/dot_general | solution.py:124
  221.0 2.8 %copy.90 = bf16[8,128,1536]{2,1,0:T(8,128)(2,1)} copy(bf16[8,128,1536]{1,2,0:T(8,128)(2,1)S(1)} %all-to-all-done.2) | data formatting | bytes 6291456 | tf_op jit(solution)/shard_map/all_to_all | solution.py:25
  223.9 3.3 %fusion.41 = (bf16[1024,768]{1,0:T(8,128)(2,1)S(1)}, bf16[1024,768]{1,0:T(8,128)(2,1)}) fusion(bf16[1024,1536]{1,0:T(8,128)(2,1)} %bitcast.118), kind=kLoop, calls=%fused_computation.61 | loop fusion | bytes 6291456 | tf_op jit(solution)/shard_map/slice | solution.py:155
  227.2 1.7 copy.91
  232.6 2.8 %fusion.43 = f32[8,1024,128]{2,1,0:T(8,128)} fusion(bf16[1024,8,96]{0,2,1:T(8,128)(2,1)S(1)} %bitcast.123, bf16[128,8,96]{0,2,1:T(8,128)(2,1)S(1)} %bitcast.131), kind=kOutput, calls=%fused_computation.63 | convolution fusion | flops 201326592 | bytes 5963776 | tf_op jit(solution)/shard_map/while/body/eval_jaxpr/ihc,jhc->hij/dot_general | solution.py:62
  236.8 6.0 %fusion.22 = bf16[8,128,96]{1,2,0:T(8,128)(2,1)} fusion(bf16[1024,8,96]{0,2,1:T(8,128)(2,1)S(1)} %bitcast.124, f32[8,1024,128]{2,1,0:T(8,128)} %fusion.43, bf16[1024,8,96]{0,2,1:T(8,128)(2,1)S(1)} %bitcast.128, bf16[128,8,96]{0,2,1:T(8,128)(2,1)} %bitcast.141, f32[8,1024]{1,0:T(8,128)} %get-tuple-element.128, f32[8,1024]{1,0:T(8,128)} %get-tuple-element.127, ...), kind=kOutput, calls=%fused_computation.28 | convolution fusion | flops 410091520 | bytes 7798912 | tf_op jit(solution)/shard_map/while/body/eval_jaxpr/hij,ihc->hjc/dot_general | solution.py:142
  242.7 1.7 copy.99
  245.8 2.7 %convolution_bitcast_fusion.1 = f32[2,768,96]{1,2,0:T(8,128)} fusion(bf16[1024,768,1]{1,0,2:T(8,128)(2,1)} %bitcast.36, bf16[2,96,1024]{2,1,0:T(8,128)(2,1)S(1)} %bitcast.140), kind=kOutput, calls=%fused_computation.26 | convolution fusion | flops 301989888 | bytes 2555904 | tf_op jit(solution)/shard_map/dot_general | solution.py:108
  248.5 3.5 %all-to-all-start.6 = ((f32[2,768,96]{1,2,0:T(8,128)}), f32[2,768,96]{1,2,0:T(8,128)S(1)}, u32[]{:S(2)}, u32[]{:S(2)}) async-start(f32[2,768,96]{1,2,0:T(8,128)} %convolution_bitcast_fusion.1), calls=%async_computation.6 | async-start | bytes 1179648 | tf_op jit(solution)/shard_map/all_to_all | solution.py:32
  252.1 3.3 %fusion.23 = bf16[8,128,96]{1,2,0:T(8,128)(2,1)S(1)} fusion(bf16[1024,8,96]{0,2,1:T(8,128)(2,1)S(1)} %bitcast.129, f32[8,1024,128]{2,1,0:T(8,128)} %fusion.43, f32[8,1024]{1,0:T(8,128)S(1)} %copy-done.18, pred[128]{0:T(512)(128)(4,1)S(1)} %add_compare_fusion), kind=kOutput, calls=%fused_computation.29 | convolution fusion | flops 205619200 | bytes 5996672 | tf_op jit(solution)/shard_map/while/body/eval_jaxpr/hij,ihc->hjc/dot_general | solution.py:145
  256.2 2.8 %all-to-all-done.6 = f32[2,768,96]{1,2,0:T(8,128)S(1)} async-done(((f32[2,768,96]{1,2,0:T(8,128)}), f32[2,768,96]{1,2,0:T(8,128)S(1)}, u32[]{:S(2)}, u32[]{:S(2)}) %all-to-all-start.6) | async-done | bytes 589856 | tf_op jit(solution)/shard_map/all_to_all | solution.py:32
  (75 shorter events, 27.6 us)
Async XLA Ops:
  3.9 8.1 %copy-start.12 = (bf16[1,128,768]{2,1,0:T(8,128)(2,1)S(1)}, bf16[1,128,768]{2,1,0:T(8,128)(2,1)}, u32[]{:S(2)}) copy-start(bf16[1,128,768]{2,1,0:T(8,128)(2,1)} %param.7) | copy-start | bytes 589828
  4.0 78.2 %all-to-all-start = ((bf16[8,128,1536]{1,2,0:T(8,128)(2,1)}), bf16[8,128,1536]{1,2,0:T(8,128)(2,1)S(1)}, u32[]{:S(2)}, u32[]{:S(2)}) async-start(bf16[8,128,1536]{1,2,0:T(8,128)(2,1)} %broadcast_in_dim.91), calls=%async_computation | async-start | bytes 6291456 | tf_op jit(solution)/shard_map/all_to_all | solution.py:25
  11.4 5.8 %copy-start.16 = (bf16[1,128,768]{2,1,0:T(8,128)(2,1)S(1)}, bf16[1,128,768]{2,1,0:T(8,128)(2,1)}, u32[]{:S(2)}) copy-start(bf16[1,128,768]{2,1,0:T(8,128)(2,1)} %param.13) | copy-start | bytes 589828
  18.0 5.7 %copy-start.13 = (bf16[1,128,768]{2,1,0:T(8,128)(2,1)S(1)}, bf16[1,128,768]{2,1,0:T(8,128)(2,1)}, u32[]{:S(2)}) copy-start(bf16[1,128,768]{2,1,0:T(8,128)(2,1)} %param.7) | copy-start | bytes 589828
  23.0 0.7 copy-start.3
  27.2 68.9 %copy-start.20 = (pred[1024]{0:T(1024)(128)(4,1)}, pred[1024]{0:T(1024)(128)(4,1)S(1)}, u32[]{:S(2)}) copy-start(pred[1024]{0:T(1024)(128)(4,1)S(1)} %iota_compare_fusion) | copy-start | bytes 3076
  82.1 25.5 %all-to-all-start.5 = ((bf16[128,8,192]{0,2,1:T(8,128)(2,1)}), bf16[128,8,192]{0,2,1:T(8,128)(2,1)S(1)}, u32[]{:S(2)}, u32[]{:S(2)}) async-start(bf16[128,8,192]{0,2,1:T(8,128)(2,1)} %bitcast.130), calls=%async_computation.5 | async-start | bytes 786432 | tf_op jit(solution)/shard_map/all_to_all | solution.py:104
  93.6 5.3 %copy-start.2 = (bf16[1024,768]{0,1:T(8,128)(2,1)}, bf16[1024,768]{0,1:T(8,128)(2,1)S(1)}, u32[]{:S(2)}) copy-start(bf16[1024,768]{0,1:T(8,128)(2,1)S(1)} %copy.79) | copy-start | bytes 4718596
  96.0 1.9 copy-start
  100.3 6.4 %copy-start.5 = (bf16[1024,768]{0,1:T(8,128)(2,1)}, bf16[1024,768]{0,1:T(8,128)(2,1)S(1)}, u32[]{:S(2)}) copy-start(bf16[1024,768]{0,1:T(8,128)(2,1)S(1)} %copy.81) | copy-start | bytes 4718596
  100.3 6.4 %copy-start.1 = (bf16[1536,768]{1,0:T(8,128)(2,1)S(1)}, bf16[1536,768]{1,0:T(8,128)(2,1)}, u32[]{:S(2)}) copy-start(bf16[1536,768]{1,0:T(8,128)(2,1)} %copy.106) | copy-start | bytes 7077892
  106.7 8.2 %copy-start.11 = (bf16[128,8,96]{0,2,1:T(8,128)(2,1)}, bf16[128,8,96]{0,2,1:T(8,128)(2,1)S(1)}, u32[]{:S(2)}) copy-start(bf16[128,8,96]{0,2,1:T(8,128)(2,1)S(1)} %get-tuple-element.135) | copy-start | bytes 589828
  106.7 6.1 %copy-start.9 = (bf16[128,1536]{0,1:T(8,128)(2,1)S(1)}, bf16[128,1536]{0,1:T(8,128)(2,1)}, u32[]{:S(2)}) copy-start(bf16[128,1536]{0,1:T(8,128)(2,1)} %copy.89) | copy-start | bytes 1179652
  107.6 5.2 %copy-start.7 = (bf16[128,8,192]{0,2,1:T(8,128)(2,1)}, bf16[128,8,192]{0,2,1:T(8,128)(2,1)S(1)}, u32[]{:S(2)}) copy-start(bf16[128,8,192]{0,2,1:T(8,128)(2,1)S(1)} %all-to-all-done.5) | copy-start | bytes 1179652
  114.9 6.1 %copy-start.4 = (bf16[128,768]{1,0:T(8,128)(2,1)S(1)}, bf16[128,768]{1,0:T(8,128)(2,1)}, u32[]{:S(2)}) copy-start(bf16[128,768]{1,0:T(8,128)(2,1)} %copy-done.3) | copy-start | bytes 589828
  114.9 77.1 %all-to-all-start.2 = ((bf16[8,128,1536]{1,2,0:T(8,128)(2,1)}), bf16[8,128,1536]{1,2,0:T(8,128)(2,1)S(1)}, u32[]{:S(2)}, u32[]{:S(2)}) async-start(bf16[8,128,1536]{1,2,0:T(8,128)(2,1)} %broadcast_in_dim.94), calls=%async_computation.2 | async-start | bytes 6291456 | tf_op jit(solution)/shard_map/all_to_all | solution.py:25
  121.1 1.2 copy-start.14
  123.0 90.7 %copy-start.8 = (bf16[128,8,192]{0,2,1:T(8,128)(2,1)S(1)}, bf16[128,8,192]{0,2,1:T(8,128)(2,1)}, u32[]{:S(2)}) copy-start(bf16[128,8,192]{0,2,1:T(8,128)(2,1)} %copy-done.7) | copy-start | bytes 1179652
  192.6 10.9 %all-to-all-start.3 = ((f32[8,16,128]{2,1,0:T(8,128)}), f32[8,16,128]{2,1,0:T(8,128)}, u32[]{:S(2)}, u32[]{:S(2)}) async-start(f32[8,16,128]{2,1,0:T(8,128)} %broadcast_in_dim.95), calls=%async_computation.3 | async-start | bytes 131072 | tf_op jit(solution)/shard_map/all_to_all | solution.py:25
  198.4 16.2 %copy-start.19 = (f32[8,128]{1,0:T(8,128)S(1)}, f32[8,128]{1,0:T(8,128)}, u32[]{:S(2)}) copy-start(f32[8,128]{1,0:T(8,128)} %get-tuple-element.129) | copy-start | bytes 12292
  198.4 16.2 %copy-start.21 = (pred[1024]{0:T(1024)(128)(4,1)S(1)}, pred[1024]{0:T(1024)(128)(4,1)}, u32[]{:S(2)}) copy-start(pred[1024]{0:T(1024)(128)(4,1)} %copy-done.20) | copy-start | bytes 3076
  205.7 40.1 %all-to-all-start.4 = ((bf16[8,128,768]{2,1,0:T(8,128)(2,1)}), bf16[8,128,768]{2,1,0:T(8,128)(2,1)}, u32[]{:S(2)}, u32[]{:S(2)}) async-start(bf16[8,128,768]{2,1,0:T(8,128)(2,1)} %broadcast_in_dim.96), calls=%async_computation.4 | async-start | bytes 3145728 | tf_op jit(solution)/shard_map/all_to_all | solution.py:25
  227.2 4.7 %copy-start.17 = (bf16[1,128,768]{2,1,0:T(8,128)(2,1)S(1)}, bf16[1,128,768]{2,1,0:T(8,128)(2,1)}, u32[]{:S(2)}) copy-start(bf16[1,128,768]{2,1,0:T(8,128)(2,1)} %param.11) | copy-start | bytes 589828
  228.9 3.7 %copy-start.10 = (bf16[1,128,768]{1,2,0:T(8,128)(2,1)S(1)}, bf16[1,128,768]{1,2,0:T(8,128)(2,1)}, u32[]{:S(2)}) copy-start(bf16[1,128,768]{1,2,0:T(8,128)(2,1)} %copy.92) | copy-start | bytes 589828
  232.6 4.2 %copy-start.6 = (bf16[1024,768]{0,1:T(8,128)(2,1)S(1)}, bf16[1024,768]{0,1:T(8,128)(2,1)}, u32[]{:S(2)}) copy-start(bf16[1024,768]{0,1:T(8,128)(2,1)} %copy.93) | copy-start | bytes 4718596
  236.7 9.1 %copy-start.15 = (bf16[1024,192]{0,1:T(8,128)(2,1)S(1)}, bf16[1024,192]{0,1:T(8,128)(2,1)}, u32[]{:S(2)}) copy-start(bf16[1024,192]{0,1:T(8,128)(2,1)} %copy_bitcast_fusion) | copy-start | bytes 1179652
  242.7 9.3 %copy-start.18 = (f32[8,1024]{1,0:T(8,128)S(1)}, f32[8,1024]{1,0:T(8,128)}, u32[]{:S(2)}) copy-start(f32[8,1024]{1,0:T(8,128)} %get-tuple-element.127) | copy-start | bytes 98308
  248.5 10.4 %all-to-all-start.6 = ((f32[2,768,96]{1,2,0:T(8,128)}), f32[2,768,96]{1,2,0:T(8,128)S(1)}, u32[]{:S(2)}, u32[]{:S(2)}) async-start(f32[2,768,96]{1,2,0:T(8,128)} %convolution_bitcast_fusion.1), calls=%async_computation.6 | async-start | bytes 1179648 | tf_op jit(solution)/shard_map/all_to_all | solution.py:32
